TPU v7x, 128 devices: a whole 4x4x4 slice. The times are simulated.
128 devices in a mesh: shot: 16 (over y_lo, z, core), freq: 8 (over y_hi, x).
Axes of the slice: x: 4, y: 4 (y_hi: 2, y_lo: 2; y = y_hi * 2 + y_lo), z: 4, core: 2. Of those that a mesh axis runs over, the one named last changes fastest.
Arguments:
- traces: bfloat16 [1024, 1024, 512], P('shot', 'freq'), may hold values from -6 to 6
Outputs:
- multiples: bfloat16 [1024, 1024, 512], P('shot', 'freq')
All inputs are finite; a program needn't handle non-finite values.
Results may differ from a plain program's by a relative error of at most 0.001.
Values sent between devices are 32-bit elements; how exact they have to be, the bound alone decides.
No kernel may reach another device: no remote copies, remote signals or barrier semaphores. Data moves between devices by JAX's collectives and lax.ppermute only.
A program may use at most 128 MiB of HBM per device.

v0:
```python
import functools

import jax
import jax.numpy as jnp
from jax import lax
from jax.experimental import pallas as pl
from jax.experimental.pallas import tpu as pltpu
from jax.sharding import PartitionSpec as P

NT = 512
NF = 128


def make_tables(count_t, count_f):
    times = jnp.arange(count_t, dtype=jnp.int32)
    bins = count_t // 32 + jnp.arange(count_f, dtype=jnp.int32)
    phase = (times[:, None] * bins[None, :] % count_t).astype(jnp.float32) * (
        2.0 * jnp.pi / count_t
    )
    ramp = float(count_t // 16)
    tval = times.astype(jnp.float32)
    taper = jnp.minimum(jnp.minimum((tval + 0.5) / ramp, (count_t - tval - 0.5) / ramp), 1.0)
    cosine = jnp.cos(phase) * taper[:, None]
    sine = jnp.sin(phase) * taper[:, None]
    forward = jnp.stack([cosine, -sine], axis=1) / jnp.sqrt(jnp.float32(count_t))
    inverse = jnp.stack([cosine.T, -sine.T], axis=1) / jnp.sqrt(jnp.float32(count_f))
    return (forward, inverse)


def split(x):
    high = x.astype(jnp.bfloat16)
    low = (x - high.astype(jnp.float32)).astype(jnp.bfloat16)
    return high, low


def product(high, low, left, right):
    dot = functools.partial(jnp.dot, preferred_element_type=jnp.float32)
    return (
        dot(high[left], high[right])
        + dot(high[left], low[right])
        + dot(low[left], high[right])
    )


def square_kernel(n_shot, n_freq, rows, cols, scale, y_ref, out_ref, high, low):
    width = out_ref.shape[1] * cols
    j = pl.program_id(0)

    @pl.when(j == 0)
    def _():
        def fill(a, carry):
            top = pl.multiple_of(a * rows, rows)
            for b in range(n_freq):
                real = y_ref[a, b, 0]
                imag = y_ref[a, b, 1]
                for index, part in enumerate((real, imag, real + imag)):
                    h, l = split(part)
                    high[index, pl.ds(top, rows), pl.ds(b * cols, cols)] = h
                    low[index, pl.ds(top, rows), pl.ds(b * cols, cols)] = l
            return carry

        lax.fori_loop(0, n_shot, fill, 0)

    start = pl.multiple_of(j * width, width)
    every = slice(None)
    block = pl.ds(start, width)

    def side(index):
        return (index, every, every), (index, every, block)

    rr = product(high, low, *side(0))
    ii = product(high, low, *side(1))
    ss = product(high, low, *side(2))
    real = (rr - ii) * scale
    imag = (ss - rr - ii) * scale
    for a in range(n_shot):
        for b in range(out_ref.shape[1]):
            tile = (slice(a * rows, (a + 1) * rows), slice(b * cols, (b + 1) * cols))
            out_ref[a, b, 0] = real[tile]
            out_ref[a, b, 1] = imag[tile]


def complex_square(blocks):
    n_shot, n_freq, _, rows, cols = blocks.shape
    order = n_shot * rows
    group = 2
    kernel = functools.partial(
        square_kernel, n_shot, n_freq, rows, cols, float(-1.0 / (order ** 0.5))
    )
    return pl.pallas_call(
        kernel,
        out_shape=jax.ShapeDtypeStruct(blocks.shape, jnp.float32),
        grid=(n_freq // group,),
        in_specs=[pl.BlockSpec(memory_space=pltpu.VMEM)],
        out_specs=pl.BlockSpec(
            (n_shot, group, 2, rows, cols), lambda j: (0, j, 0, 0, 0)
        ),
        scratch_shapes=[
            pltpu.VMEM((3, order, n_freq * cols), jnp.bfloat16),
            pltpu.VMEM((3, order, n_freq * cols), jnp.bfloat16),
        ],
        compiler_params=pltpu.CompilerParams(
            dimension_semantics=("arbitrary",), vmem_limit_bytes=60 * 1024 * 1024
        ),
    )(blocks)


def per_device(traces):
    forward, inverse = make_tables(NT, NF)
    spectra = jnp.einsum(
        "srt,tpb->bpsr",
        traces.astype(jnp.float32),
        forward,
        precision=lax.Precision.HIGH,
        preferred_element_type=jnp.float32,
    )
    rows = traces.shape[0]
    cols = traces.shape[1]
    n_shot = lax.axis_size("shot")
    n_freq = lax.axis_size("freq")
    moved = lax.all_to_all(spectra[None], ("shot", "freq"), split_axis=1, concat_axis=0, tiled=True)
    local_bins = moved.shape[-4]
    assert local_bins == 1
    blocks = moved.reshape(n_shot, n_freq, 2, rows, cols)
    pred = complex_square(blocks)
    home = lax.all_to_all(
        pred.reshape(n_shot * n_freq, 1, 2, rows, cols),
        ("shot", "freq"),
        split_axis=0,
        concat_axis=1,
        tiled=True,
    )
    home = home.reshape(n_shot * n_freq, 2, rows, cols)
    result = jnp.einsum(
        "bpsr,bpt->srt",
        home,
        inverse,
        precision=lax.Precision.HIGH,
        preferred_element_type=jnp.float32,
    )
    return result.astype(jnp.bfloat16)


def solution(mesh):
    return jax.shard_map(
        per_device,
        mesh=mesh,
        in_specs=(P("shot", "freq", None),),
        out_specs=P("shot", "freq", None),
        check_vma=False,
    )
```

profile of v0, /device:TPU:6, one launch (start us, length us, event | category | flops | bytes accessed | tf_op | source)
XLA Modules:
  0.0 307.9 jit_solution(2505341292475774048)
XLA Ops:
  0.0 1.1 cosine_multiply_fusion.1
  1.1 7.3 %fusion.3 = f32[1,128,2,64,128]{4,1,3,2,0:T(8,128)S(1)} fusion(bf16[64,128,512]{2,1,0:T(8,128)(2,1)} %param.1, f32[512,1,128]{0,2,1:T(8,128)S(1)} %get-tuple-element.8, f32[512,1,128]{0,2,1:T(8,128)S(1)} %get-tuple-element.7), kind=kOutput, calls=%fused_computation.4 | convolution fusion | flops 6442713088 | bytes 17301504 | tf_op jit(solution)/shard_map/srt,tpb->bpsr/dot_general | solution.py:110
  8.5 4.9 %copy.4 = f32[1,128,2,64,128]{4,3,2,0,1:T(8,128)S(1)} copy(f32[1,128,2,64,128]{4,1,3,2,0:T(8,128)S(1)} %fusion.3) | data formatting | bytes 16777216 | tf_op jit(solution)/shard_map/broadcast_in_dim | solution.py:121
  13.3 109.8 %all_to_all.8 = f32[1,128,2,64,128]{4,3,2,0,1:T(8,128)} all-to-all(f32[1,128,2,64,128]{4,3,2,0,1:T(8,128)S(1)} %copy.4), channel_id=1, replica_groups=mesh['shot'=16,'freq'=8] {'shot','freq'}, dimensions={1} | all-to-all | bytes 16777216 | tf_op jit(solution)/shard_map/all_to_all | solution.py:121
  123.1 28.0 %shard_map.17 = f32[16,8,2,64,128]{4,3,2,1,0:T(8,128)} custom-call(f32[16,8,2,64,128]{4,3,2,1,0:T(8,128)} %bitcast.25), custom_call_target="tpu_custom_call" | custom-call | tf_op jit(solution)/shard_map/pallas_call | solution.py:90
  151.1 15.3 %copy.5 = f32[128,1,2,64,128]{4,2,3,1,0:T(2,128)} copy(f32[128,1,2,64,128]{4,3,2,0,1:T(8,128)} %bitcast.26) | data formatting | bytes 16777216 | tf_op jit(solution)/shard_map/reshape | solution.py:127
  166.4 5.0 %all-to-all-start.1 = ((f32[128,1,2,64,128]{4,2,3,1,0:T(2,128)}), f32[128,1,2,64,128]{4,2,3,1,0:T(2,128)}, u32[]{:S(2)}, u32[]{:S(2)}) async-start(f32[128,1,2,64,128]{4,2,3,1,0:T(2,128)} %copy.5), calls=%async_computation.1 | async-start | bytes 16777216 | tf_op jit(solution)/shard_map/all_to_all | solution.py:126
  171.5 1.1 cosine_multiply_fusion
  172.6 110.8 %all-to-all-done.1 = f32[128,1,2,64,128]{4,2,3,1,0:T(2,128)} async-done(((f32[128,1,2,64,128]{4,2,3,1,0:T(2,128)}), f32[128,1,2,64,128]{4,2,3,1,0:T(2,128)}, u32[]{:S(2)}, u32[]{:S(2)}) %all-to-all-start.1) | async-done | bytes 8388640 | tf_op jit(solution)/shard_map/all_to_all | solution.py:126
  283.4 13.3 %copy.6 = f32[128,1,2,64,128]{0,4,2,3,1:T(8,128)} copy(f32[128,1,2,64,128]{4,2,3,1,0:T(2,128)} %all-to-all-done.1) | data formatting | bytes 16777216 | tf_op jit(solution)/shard_map/all_to_all | solution.py:126
  296.7 11.2 %bitcast_convert_fusion = bf16[64,128,512]{2,1,0:T(8,128)(2,1)} fusion(f32[128,1,2,64,128]{0,4,2,3,1:T(8,128)} %copy.6, f32[128,1,512]{2,0,1:T(8,128)S(1)} %get-tuple-element.6, f32[128,1,512]{2,0,1:T(8,128)S(1)} %get-tuple-element.5), kind=kOutput, calls=%fused_computation | convolution fusion | flops 6446907392 | bytes 17301504 | tf_op jit(solution)/shard_map/bpsr,bpt->srt/dot_general | solution.py:134
  (2 shorter events, 0.0 us)
Async XLA Ops:
  166.4 116.9 %all-to-all-start.1 = ((f32[128,1,2,64,128]{4,2,3,1,0:T(2,128)}), f32[128,1,2,64,128]{4,2,3,1,0:T(2,128)}, u32[]{:S(2)}, u32[]{:S(2)}) async-start(f32[128,1,2,64,128]{4,2,3,1,0:T(2,128)} %copy.5), calls=%async_computation.1 | async-start | bytes 16777216 | tf_op jit(solution)/shard_map/all_to_all | solution.py:126
where the time goes:
time: 309 us; the launch traced here: 308 us
  waiting for transfers between devices  111 us (36%)
  blocking collectives  110 us (36%)
  local copies, waits for them, and re-layouts  33.5 us (11%)
  Pallas kernels  28 us (9%)
  matrix products  18.5 us (6%)
  starting transfers between devices  5.05 us (2%)
    all_to_all x1, waiting for transfers between devices, per_device(): lax.all_to_all(pred.reshape(n_shot * n_freq, 1, 2, rows, cols), ('shot',...  111 us
    all_to_all x1, blocking collectives, per_device(): lax.all_to_all(spectra[None], ('shot', 'freq'), split_axis=1, concat_axis...  110 us
    pallas_call x1, Pallas kernels, complex_square(): pl.pallas_call(kernel, out_shape=jax.ShapeDtypeStruct(blocks.shape, jnp.f...  28 us
    reshape x1, local copies, waits for them, and re-layouts, per_device(): pred.reshape(n_shot * n_freq, 1, 2, rows, cols)  15.3 us
    all_to_all x1, local copies, waits for them, and re-layouts, per_device(): lax.all_to_all(pred.reshape(n_shot * n_freq, 1, 2, rows, cols), ('shot',...  13.3 us
    dot_general x1, matrix products, per_device(): jnp.einsum('bpsr,bpt->srt', home, inverse, precision=lax.Precision.HIGH,...  11.2 us
    dot_general x1, matrix products, per_device(): jnp.einsum('srt,tpb->bpsr', traces.astype(jnp.float32), forward, precisio...  7.32 us
  transfers between devices with their start and end apart: 1, of which 1 were waited for; matrix products, arithmetic and copies ran while one was open for 0% of the time, Pallas kernels for 0%

commit v1 on v0

--- a/solution.py
+++ b/solution.py
@@ -31,6 +31,11 @@
     high = x.astype(jnp.bfloat16)
     low = (x - high.astype(jnp.float32)).astype(jnp.bfloat16)
     return high, low
+
+
+def split_outside(x):
+    high = lax.reduce_precision(x, exponent_bits=8, mantissa_bits=7)
+    return high.astype(jnp.bfloat16), (x - high).astype(jnp.bfloat16)
 
 
 def product(high, low, left, right):
@@ -105,6 +110,39 @@
     )(blocks)
 
 
+def inverse_kernel(group, w_high, w_low, x_ref, out_ref):
+    n_bins, parts, _, cols = x_ref.shape
+    pieces = []
+    for s in range(group):
+        piece = x_ref[:, :, s, :].reshape(n_bins * parts, cols)
+        pieces.append(piece.T)
+    stacked = jnp.concatenate(pieces, axis=0)
+    high, low = split(stacked)
+    dot = functools.partial(jnp.dot, preferred_element_type=jnp.float32)
+    total = dot(high, w_high[...]) + dot(high, w_low[...]) + dot(low, w_high[...])
+    out_ref[...] = total.reshape(out_ref.shape).astype(out_ref.dtype)
+
+
+def inverse_transform(home, inverse):
+    n_bins, parts, rows, cols = home.shape
+    steps = inverse.shape[-1]
+    table = inverse.reshape(n_bins * parts, steps)
+    w_high, w_low = split_outside(table)
+    group = 8
+    return pl.pallas_call(
+        functools.partial(inverse_kernel, group),
+        out_shape=jax.ShapeDtypeStruct((rows, cols, steps), jnp.bfloat16),
+        grid=(rows // group,),
+        in_specs=[
+            pl.BlockSpec((n_bins * parts, steps), lambda i: (0, 0)),
+            pl.BlockSpec((n_bins * parts, steps), lambda i: (0, 0)),
+            pl.BlockSpec((n_bins, parts, group, cols), lambda i: (0, 0, i, 0)),
+        ],
+        out_specs=pl.BlockSpec((group, cols, steps), lambda i: (i, 0, 0)),
+        compiler_params=pltpu.CompilerParams(dimension_semantics=("arbitrary",)),
+    )(w_high, w_low, home)
+
+
 def per_device(traces):
     forward, inverse = make_tables(NT, NF)
     spectra = jnp.einsum(
@@ -124,21 +162,14 @@
     blocks = moved.reshape(n_shot, n_freq, 2, rows, cols)
     pred = complex_square(blocks)
     home = lax.all_to_all(
-        pred.reshape(n_shot * n_freq, 1, 2, rows, cols),
+        pred.reshape(1, n_shot * n_freq, 2, rows, cols),
         ("shot", "freq"),
-        split_axis=0,
-        concat_axis=1,
+        split_axis=1,
+        concat_axis=0,
         tiled=True,
     )
     home = home.reshape(n_shot * n_freq, 2, rows, cols)
-    result = jnp.einsum(
-        "bpsr,bpt->srt",
-        home,
-        inverse,
-        precision=lax.Precision.HIGH,
-        preferred_element_type=jnp.float32,
-    )
-    return result.astype(jnp.bfloat16)
+    return inverse_transform(home, inverse)
 
 
 def solution(mesh):

time: 309 us -> 283 us (0.916)
  local copies, waits for them, and re-layouts: 33.5 us -> 5.62 us
  Pallas kernels: 28 us -> 42 us
  matrix products: 18.5 us -> 7.32 us
    reshape x1 -> x0, local copies, waits for them, and re-layouts: 15.3 us -> none  [per_device(): pred.reshape(n_shot * n_freq, 1, 2, rows, cols)]
    pallas_call x0 -> x1, Pallas kernels: none -> 14.1 us  [inverse_transform(): pl.pallas_call(functools.partial(inverse_kernel, group), out_shape=jax.Sh...]
    all_to_all x1 -> x0, local copies, waits for them, and re-layouts: 13.3 us -> none  [per_device(): lax.all_to_all(pred.reshape(n_shot * n_freq, 1, 2, rows, cols), ('shot',...]
    dot_general x1 -> x0, matrix products: 11.2 us -> none  [per_device(): jnp.einsum('bpsr,bpt->srt', home, inverse, precision=lax.Precision.HIGH,...]
  transfers between devices with their start and end apart: 1 -> 1, of which waited for: 1 -> 1; matrix products, arithmetic and copies ran while one was open for 0% -> 1% of each run, Pallas kernels for 0% -> 0%
where the time goes in v1:
time: 283 us; the launch traced here: 282 us
  blocking collectives  110 us (39%)
  waiting for transfers between devices  109 us (39%)
  Pallas kernels  42 us (15%)
  matrix products  7.32 us (3%)
  local copies, waits for them, and re-layouts  5.62 us (2%)
  starting transfers between devices  5.05 us (2%)
  other arithmetic  3.22 us (1%)
    all_to_all x1, blocking collectives, per_device(): lax.all_to_all(spectra[None], ('shot', 'freq'), split_axis=1, concat_axis...  110 us
    all_to_all x1, waiting for transfers between devices, per_device(): lax.all_to_all(pred.reshape(1, n_shot * n_freq, 2, rows, cols), ('shot',...  109 us
    pallas_call x1, Pallas kernels, complex_square(): pl.pallas_call(kernel, out_shape=jax.ShapeDtypeStruct(blocks.shape, jnp.f...  28 us
    pallas_call x1, Pallas kernels, inverse_transform(): pl.pallas_call(functools.partial(inverse_kernel, group), out_shape=jax.Sh...  14.1 us
    dot_general x1, matrix products, per_device(): jnp.einsum('srt,tpb->bpsr', traces.astype(jnp.float32), forward, precisio...  7.32 us
  transfers between devices with their start and end apart: 1, of which 1 were waited for; matrix products, arithmetic and copies ran while one was open for 1% of the time, Pallas kernels for 0%

profile of v1, /device:TPU:6, one launch (start us, length us, event | category | flops | bytes accessed | tf_op | source)
XLA Modules:
  0.0 282.1 jit_solution(17169969979183121364)
XLA Ops:
  0.0 1.1 cosine_multiply_fusion
  1.1 7.3 %fusion.2 = f32[1,128,2,64,128]{4,1,3,2,0:T(8,128)S(1)} fusion(bf16[64,128,512]{2,1,0:T(8,128)(2,1)} %param.1, f32[512,1,128]{0,2,1:T(8,128)S(1)} %get-tuple-element.8, f32[512,1,128]{0,2,1:T(8,128)S(1)} %get-tuple-element.7), kind=kOutput, calls=%fused_computation.2 | convolution fusion | flops 6442713088 | bytes 17301504 | tf_op jit(solution)/shard_map/srt,tpb->bpsr/dot_general | solution.py:148
  8.5 4.9 %copy.6 = f32[1,128,2,64,128]{4,3,2,0,1:T(8,128)S(1)} copy(f32[1,128,2,64,128]{4,1,3,2,0:T(8,128)S(1)} %fusion.2) | data formatting | bytes 16777216 | tf_op jit(solution)/shard_map/broadcast_in_dim | solution.py:159
  13.3 109.8 %all_to_all.8 = f32[1,128,2,64,128]{4,3,2,0,1:T(8,128)} all-to-all(f32[1,128,2,64,128]{4,3,2,0,1:T(8,128)S(1)} %copy.6), channel_id=1, replica_groups=mesh['shot'=16,'freq'=8] {'shot','freq'}, dimensions={1} | all-to-all | bytes 16777216 | tf_op jit(solution)/shard_map/all_to_all | solution.py:159
  123.1 28.0 %shard_map.17 = f32[16,8,2,64,128]{4,3,2,1,0:T(8,128)} custom-call(f32[16,8,2,64,128]{4,3,2,1,0:T(8,128)} %bitcast.20), custom_call_target="tpu_custom_call" | custom-call | tf_op jit(solution)/shard_map/pallas_call | solution.py:95
  151.1 5.0 %all-to-all-start.1 = ((f32[1,128,2,64,128]{4,3,2,0,1:T(8,128)}), f32[1,128,2,64,128]{4,3,2,0,1:T(8,128)}, u32[]{:S(2)}, u32[]{:S(2)}) async-start(f32[1,128,2,64,128]{4,3,2,0,1:T(8,128)} %bitcast.19), calls=%async_computation.1 | async-start | bytes 16777216 | tf_op jit(solution)/shard_map/all_to_all | solution.py:164
  156.2 1.1 cosine_multiply_fusion.1
  157.3 0.1 maximum_multiply_fusion
  157.4 0.4 copy.5
  157.8 0.4 div.36
  158.1 0.9 fusion.5
  159.1 109.0 %all-to-all-done.1 = f32[1,128,2,64,128]{4,3,2,0,1:T(8,128)} async-done(((f32[1,128,2,64,128]{4,3,2,0,1:T(8,128)}), f32[1,128,2,64,128]{4,3,2,0,1:T(8,128)}, u32[]{:S(2)}, u32[]{:S(2)}) %all-to-all-start.1) | async-done | bytes 8388640 | tf_op jit(solution)/shard_map/all_to_all | solution.py:164
  268.1 14.1 %shard_map.18 = bf16[64,128,512]{2,1,0:T(8,128)(2,1)} custom-call(bf16[256,512]{1,0:T(8,128)(2,1)} %get-tuple-element.6.w_high, bf16[256,512]{1,0:T(8,128)(2,1)} %get-tuple-element.5.w_low, f32[128,2,64,128]{3,2,1,0:T(8,128)} %bitcast.8.x_ref), custom_call_target="tpu_custom_call" | custom-call | tf_op jit(solution)/shard_map/pallas_call | solution.py:132
  (2 shorter events, 0.0 us)
Async XLA Ops:
  151.1 116.9 %all-to-all-start.1 = ((f32[1,128,2,64,128]{4,3,2,0,1:T(8,128)}), f32[1,128,2,64,128]{4,3,2,0,1:T(8,128)}, u32[]{:S(2)}, u32[]{:S(2)}) async-start(f32[1,128,2,64,128]{4,3,2,0,1:T(8,128)} %bitcast.19), calls=%async_computation.1 | async-start | bytes 16777216 | tf_op jit(solution)/shard_map/all_to_all | solution.py:164

commit v2 on v1

--- a/solution.py
+++ b/solution.py
@@ -143,15 +143,41 @@
     )(w_high, w_low, home)
 
 
+def forward_kernel(group, w_high, w_low, x_ref, out_ref):
+    _, cols, steps = x_ref.shape
+    flat = x_ref[...].reshape(group * cols, steps)
+    dims = (((1,), (1,)), ((), ()))
+    dot = functools.partial(lax.dot_general, dimension_numbers=dims, preferred_element_type=jnp.float32)
+    total = dot(w_high[...], flat) + dot(w_low[...], flat)
+    n_bins, parts = out_ref.shape[0], out_ref.shape[1]
+    for s in range(group):
+        piece = total[:, s * cols:(s + 1) * cols].reshape(n_bins, parts, cols)
+        out_ref[:, :, s, :] = piece
+
+
+def forward_transform(traces, forward):
+    rows, cols, steps = traces.shape
+    parts, n_bins = forward.shape[1], forward.shape[2]
+    table = forward.transpose(2, 1, 0).reshape(n_bins * parts, steps)
+    w_high, w_low = split_outside(table)
+    group = 8
+    return pl.pallas_call(
+        functools.partial(forward_kernel, group),
+        out_shape=jax.ShapeDtypeStruct((n_bins, parts, rows, cols), jnp.float32),
+        grid=(rows // group,),
+        in_specs=[
+            pl.BlockSpec((n_bins * parts, steps), lambda i: (0, 0)),
+            pl.BlockSpec((n_bins * parts, steps), lambda i: (0, 0)),
+            pl.BlockSpec((group, cols, steps), lambda i: (i, 0, 0)),
+        ],
+        out_specs=pl.BlockSpec((n_bins, parts, group, cols), lambda i: (0, 0, i, 0)),
+        compiler_params=pltpu.CompilerParams(dimension_semantics=("arbitrary",)),
+    )(w_high, w_low, traces)
+
+
 def per_device(traces):
     forward, inverse = make_tables(NT, NF)
-    spectra = jnp.einsum(
-        "srt,tpb->bpsr",
-        traces.astype(jnp.float32),
-        forward,
-        precision=lax.Precision.HIGH,
-        preferred_element_type=jnp.float32,
-    )
+    spectra = forward_transform(traces, forward)
     rows = traces.shape[0]
     cols = traces.shape[1]
     n_shot = lax.axis_size("shot")

time: 283 us -> 286 us (1.011)
  Pallas kernels: 42 us -> 55.1 us
  matrix products: 7.32 us -> 0 us
  local copies, waits for them, and re-layouts: 5.62 us -> 1.36 us
    pallas_call x0 -> x1, Pallas kernels: none -> 13 us  [forward_transform(): pl.pallas_call(functools.partial(forward_kernel, group), out_shape=jax.Sh...]
    dot_general x1 -> x0, matrix products: 7.32 us -> none  [per_device(): jnp.einsum('srt,tpb->bpsr', traces.astype(jnp.float32), forward, precisio...]
    broadcast_in_dim x1 -> x0, local copies, waits for them, and re-layouts: 4.86 us -> none  [per_device(): spectra[None]]
where the time goes in v2:
time: 286 us; the launch traced here: 285 us
  blocking collectives  110 us (38%)
  waiting for transfers between devices  109 us (38%)
  Pallas kernels  55.1 us (19%)
  starting transfers between devices  5.06 us (2%)
  other arithmetic  4.08 us (1%)
    all_to_all x1, blocking collectives, per_device(): lax.all_to_all(spectra[None], ('shot', 'freq'), split_axis=1, concat_axis...  110 us
    all_to_all x1, waiting for transfers between devices, per_device(): lax.all_to_all(pred.reshape(1, n_shot * n_freq, 2, rows, cols), ('shot',...  109 us
    pallas_call x1, Pallas kernels, complex_square(): pl.pallas_call(kernel, out_shape=jax.ShapeDtypeStruct(blocks.shape, jnp.f...  28 us
    pallas_call x1, Pallas kernels, inverse_transform(): pl.pallas_call(functools.partial(inverse_kernel, group), out_shape=jax.Sh...  14.1 us
    pallas_call x1, Pallas kernels, forward_transform(): pl.pallas_call(functools.partial(forward_kernel, group), out_shape=jax.Sh...  13 us
  transfers between devices with their start and end apart: 1, of which 1 were waited for; matrix products, arithmetic and copies ran while one was open for 1% of the time, Pallas kernels for 0%

profile of v2, /device:TPU:6, one launch (start us, length us, event | category | flops | bytes accessed | tf_op | source)
XLA Modules:
  0.0 284.7 jit_solution(18196568754991977561)
XLA Ops:
  0.0 1.1 cosine_multiply_fusion
  1.1 0.2 copy.5
  1.4 0.4 reshape.318
  1.7 0.9 fusion.1
  2.6 13.0 %shard_map.17 = f32[128,2,64,128]{3,2,1,0:T(8,128)} custom-call(bf16[256,512]{1,0:T(8,128)(2,1)} %get-tuple-element.6.w_high, bf16[256,512]{1,0:T(8,128)(2,1)} %get-tuple-element.5.w_low, bf16[64,128,512]{2,1,0:T(8,128)(2,1)} %x_ref.1), custom_call_target="tpu_custom_call" | custom-call | tf_op jit(solution)/shard_map/pallas_call | solution.py:164
  15.6 110.1 %all_to_all.8 = f32[1,128,2,64,128]{4,3,2,0,1:T(8,128)} all-to-all(f32[1,128,2,64,128]{4,3,2,0,1:T(8,128)} %bitcast.11), channel_id=1, replica_groups=mesh['shot'=16,'freq'=8] {'shot','freq'}, dimensions={1} | all-to-all | bytes 16777216 | tf_op jit(solution)/shard_map/all_to_all | solution.py:185
  125.8 28.0 %shard_map.18 = f32[16,8,2,64,128]{4,3,2,1,0:T(8,128)} custom-call(f32[16,8,2,64,128]{4,3,2,1,0:T(8,128)} %bitcast.12), custom_call_target="tpu_custom_call" | custom-call | tf_op jit(solution)/shard_map/pallas_call | solution.py:95
  153.7 5.1 %all-to-all-start.1 = ((f32[1,128,2,64,128]{4,3,2,0,1:T(8,128)}), f32[1,128,2,64,128]{4,3,2,0,1:T(8,128)}, u32[]{:S(2)}, u32[]{:S(2)}) async-start(f32[1,128,2,64,128]{4,3,2,0,1:T(8,128)} %bitcast.10), calls=%async_computation.1 | async-start | bytes 16777216 | tf_op jit(solution)/shard_map/all_to_all | solution.py:190
  158.8 1.1 cosine_multiply_fusion.1
  159.9 0.1 maximum_multiply_fusion
  160.0 0.4 copy.4
  160.4 0.4 div.36
  160.8 0.9 fusion
  161.7 108.9 %all-to-all-done.1 = f32[1,128,2,64,128]{4,3,2,0,1:T(8,128)} async-done(((f32[1,128,2,64,128]{4,3,2,0,1:T(8,128)}), f32[1,128,2,64,128]{4,3,2,0,1:T(8,128)}, u32[]{:S(2)}, u32[]{:S(2)}) %all-to-all-start.1) | async-done | bytes 8388640 | tf_op jit(solution)/shard_map/all_to_all | solution.py:190
  270.6 14.1 %shard_map.19 = bf16[64,128,512]{2,1,0:T(8,128)(2,1)} custom-call(bf16[256,512]{1,0:T(8,128)(2,1)} %get-tuple-element.8.w_high, bf16[256,512]{1,0:T(8,128)(2,1)} %get-tuple-element.7.w_low, f32[128,2,64,128]{3,2,1,0:T(8,128)} %bitcast.6.x_ref), custom_call_target="tpu_custom_call" | custom-call | tf_op jit(solution)/shard_map/pallas_call | solution.py:132
  (3 shorter events, 0.1 us)
Async XLA Ops:
  153.7 116.9 %all-to-all-start.1 = ((f32[1,128,2,64,128]{4,3,2,0,1:T(8,128)}), f32[1,128,2,64,128]{4,3,2,0,1:T(8,128)}, u32[]{:S(2)}, u32[]{:S(2)}) async-start(f32[1,128,2,64,128]{4,3,2,0,1:T(8,128)} %bitcast.10), calls=%async_computation.1 | async-start | bytes 16777216 | tf_op jit(solution)/shard_map/all_to_all | solution.py:190

commit v3 on v1

--- a/solution.py
+++ b/solution.py
@@ -9,6 +9,7 @@
 
 NT = 512
 NF = 128
+PARTS = 2
 
 
 def make_tables(count_t, count_f):
@@ -38,17 +39,9 @@
     return high.astype(jnp.bfloat16), (x - high).astype(jnp.bfloat16)
 
 
-def product(high, low, left, right):
-    dot = functools.partial(jnp.dot, preferred_element_type=jnp.float32)
-    return (
-        dot(high[left], high[right])
-        + dot(high[left], low[right])
-        + dot(low[left], high[right])
-    )
-
-
-def square_kernel(n_shot, n_freq, rows, cols, scale, y_ref, out_ref, high, low):
+def square_kernel(n_shot, n_freq, rows, cols, scale, part, y_ref, out_ref, high, low):
     width = out_ref.shape[1] * cols
+    span = out_ref.shape[3]
     j = pl.program_id(0)
 
     @pl.when(j == 0)
@@ -58,8 +51,8 @@
             for b in range(n_freq):
                 real = y_ref[a, b, 0]
                 imag = y_ref[a, b, 1]
-                for index, part in enumerate((real, imag, real + imag)):
-                    h, l = split(part)
+                for index, value in enumerate((real, imag, real + imag)):
+                    h, l = split(value)
                     high[index, pl.ds(top, rows), pl.ds(b * cols, cols)] = h
                     low[index, pl.ds(top, rows), pl.ds(b * cols, cols)] = l
             return carry
@@ -67,38 +60,47 @@
         lax.fori_loop(0, n_shot, fill, 0)
 
     start = pl.multiple_of(j * width, width)
-    every = slice(None)
     block = pl.ds(start, width)
-
-    def side(index):
-        return (index, every, every), (index, every, block)
-
-    rr = product(high, low, *side(0))
-    ii = product(high, low, *side(1))
-    ss = product(high, low, *side(2))
+    dot = functools.partial(jnp.dot, preferred_element_type=jnp.float32)
+
+    def product(index):
+        def left(ref):
+            return jnp.concatenate(
+                [ref[index, pl.ds(a * rows + part * span, span), :] for a in range(n_shot)],
+                axis=0,
+            )
+
+        lh, ll = left(high), left(low)
+        rh, rl = high[index, :, block], low[index, :, block]
+        return dot(lh, rh) + dot(lh, rl) + dot(ll, rh)
+
+    rr = product(0)
+    ii = product(1)
+    ss = product(2)
     real = (rr - ii) * scale
     imag = (ss - rr - ii) * scale
     for a in range(n_shot):
         for b in range(out_ref.shape[1]):
-            tile = (slice(a * rows, (a + 1) * rows), slice(b * cols, (b + 1) * cols))
+            tile = (slice(a * span, (a + 1) * span), slice(b * cols, (b + 1) * cols))
             out_ref[a, b, 0] = real[tile]
             out_ref[a, b, 1] = imag[tile]
 
 
-def complex_square(blocks):
+def complex_square(blocks, part, parts):
     n_shot, n_freq, _, rows, cols = blocks.shape
     order = n_shot * rows
+    span = rows // parts
     group = 2
     kernel = functools.partial(
-        square_kernel, n_shot, n_freq, rows, cols, float(-1.0 / (order ** 0.5))
+        square_kernel, n_shot, n_freq, rows, cols, float(-1.0 / (order ** 0.5)), part
     )
     return pl.pallas_call(
         kernel,
-        out_shape=jax.ShapeDtypeStruct(blocks.shape, jnp.float32),
+        out_shape=jax.ShapeDtypeStruct((n_shot, n_freq, 2, span, cols), jnp.float32),
         grid=(n_freq // group,),
         in_specs=[pl.BlockSpec(memory_space=pltpu.VMEM)],
         out_specs=pl.BlockSpec(
-            (n_shot, group, 2, rows, cols), lambda j: (0, j, 0, 0, 0)
+            (n_shot, group, 2, span, cols), lambda j: (0, j, 0, 0, 0)
         ),
         scratch_shapes=[
             pltpu.VMEM((3, order, n_freq * cols), jnp.bfloat16),
@@ -123,24 +125,39 @@
     out_ref[...] = total.reshape(out_ref.shape).astype(out_ref.dtype)
 
 
-def inverse_transform(home, inverse):
-    n_bins, parts, rows, cols = home.shape
+def inverse_transform(home, inverse, part, parts, previous):
+    n_bins, _, span, cols = home.shape
     steps = inverse.shape[-1]
-    table = inverse.reshape(n_bins * parts, steps)
+    table = inverse.reshape(n_bins * 2, steps)
     w_high, w_low = split_outside(table)
     group = 8
+    offset = part * (span // group)
+    operands = [w_high, w_low, home]
+    in_specs = [
+        pl.BlockSpec((n_bins * 2, steps), lambda i: (0, 0)),
+        pl.BlockSpec((n_bins * 2, steps), lambda i: (0, 0)),
+        pl.BlockSpec((n_bins, 2, group, cols), lambda i: (0, 0, i, 0)),
+    ]
+    aliases = {}
+    kernel = functools.partial(inverse_kernel, group)
+    if previous is not None:
+        operands.append(previous)
+        in_specs.append(pl.BlockSpec(memory_space=pl.ANY))
+        aliases = {3: 0}
+        kernel = functools.partial(inverse_kernel_into, group)
     return pl.pallas_call(
-        functools.partial(inverse_kernel, group),
-        out_shape=jax.ShapeDtypeStruct((rows, cols, steps), jnp.bfloat16),
-        grid=(rows // group,),
-        in_specs=[
-            pl.BlockSpec((n_bins * parts, steps), lambda i: (0, 0)),
-            pl.BlockSpec((n_bins * parts, steps), lambda i: (0, 0)),
-            pl.BlockSpec((n_bins, parts, group, cols), lambda i: (0, 0, i, 0)),
-        ],
-        out_specs=pl.BlockSpec((group, cols, steps), lambda i: (i, 0, 0)),
+        kernel,
+        out_shape=jax.ShapeDtypeStruct((span * parts, cols, steps), jnp.bfloat16),
+        grid=(span // group,),
+        in_specs=in_specs,
+        out_specs=pl.BlockSpec((group, cols, steps), lambda i: (i + offset, 0, 0)),
+        input_output_aliases=aliases,
         compiler_params=pltpu.CompilerParams(dimension_semantics=("arbitrary",)),
-    )(w_high, w_low, home)
+    )(*operands)
+
+
+def inverse_kernel_into(group, w_high, w_low, x_ref, previous_ref, out_ref):
+    inverse_kernel(group, w_high, w_low, x_ref, out_ref)
 
 
 def per_device(traces):
@@ -160,16 +177,20 @@
     local_bins = moved.shape[-4]
     assert local_bins == 1
     blocks = moved.reshape(n_shot, n_freq, 2, rows, cols)
-    pred = complex_square(blocks)
-    home = lax.all_to_all(
-        pred.reshape(1, n_shot * n_freq, 2, rows, cols),
-        ("shot", "freq"),
-        split_axis=1,
-        concat_axis=0,
-        tiled=True,
-    )
-    home = home.reshape(n_shot * n_freq, 2, rows, cols)
-    return inverse_transform(home, inverse)
+    result = None
+    for part in range(PARTS):
+        pred = complex_square(blocks, part, PARTS)
+        span = pred.shape[3]
+        home = lax.all_to_all(
+            pred.reshape(1, n_shot * n_freq, 2, span, cols),
+            ("shot", "freq"),
+            split_axis=1,
+            concat_axis=0,
+            tiled=True,
+        )
+        home = home.reshape(n_shot * n_freq, 2, span, cols)
+        result = inverse_transform(home, inverse, part, PARTS, result)
+    return result
 
 
 def solution(mesh):

time: 283 us -> 267 us (0.943)
  waiting for transfers between devices: 109 us -> 74.3 us
  Pallas kernels: 42 us -> 52.2 us
  starting transfers between devices: 5.05 us -> 11.9 us
    all_to_all x1 -> x2, waiting for transfers between devices: 109 us -> 74.3 us  [per_device(): lax.all_to_all(pred.reshape(1, n_shot * n_freq, 2, span, cols), ('shot',...]
    pallas_call x2 -> x4, Pallas kernels: 42 us -> 52.2 us  [the longest x2 36.1 us: complex_square(): pl.pallas_call(kernel, out_shape=jax.ShapeDtypeStruct((n_shot, n_freq, 2,...]
    all_to_all x1 -> x2, starting transfers between devices: 5.05 us -> 11.9 us  [per_device(): lax.all_to_all(pred.reshape(1, n_shot * n_freq, 2, span, cols), ('shot',...]
  transfers between devices with their start and end apart: 1 -> 2, of which waited for: 1 -> 2; matrix products, arithmetic and copies ran while one was open for 1% -> 1% of each run, Pallas kernels for 0% -> 10%
where the time goes in v3:
time: 267 us; the launch traced here: 264 us
  blocking collectives  110 us (41%)
  waiting for transfers between devices  74.3 us (28%)
  Pallas kernels  52.2 us (20%)
  starting transfers between devices  11.9 us (4%)
  matrix products  7.32 us (3%)
  local copies, waits for them, and re-layouts  5.62 us (2%)
  other arithmetic  3.2 us (1%)
    all_to_all x1, blocking collectives, per_device(): lax.all_to_all(spectra[None], ('shot', 'freq'), split_axis=1, concat_axis...  110 us
    all_to_all x2, waiting for transfers between devices, per_device(): lax.all_to_all(pred.reshape(1, n_shot * n_freq, 2, span, cols), ('shot',...  74.3 us
    pallas_call x2, Pallas kernels, complex_square(): pl.pallas_call(kernel, out_shape=jax.ShapeDtypeStruct((n_shot, n_freq, 2,...  36.1 us
    pallas_call x2, Pallas kernels, inverse_transform(): pl.pallas_call(kernel, out_shape=jax.ShapeDtypeStruct((span * parts, cols...  16.1 us
    all_to_all x2, starting transfers between devices, per_device(): lax.all_to_all(pred.reshape(1, n_shot * n_freq, 2, span, cols), ('shot',...  11.9 us
    dot_general x1, matrix products, per_device(): jnp.einsum('srt,tpb->bpsr', traces.astype(jnp.float32), forward, precisio...  7.32 us
  transfers between devices with their start and end apart: 2, of which 2 were waited for; matrix products, arithmetic and copies ran while one was open for 1% of the time, Pallas kernels for 10%

profile of v3, /device:TPU:6, one launch (start us, length us, event | category | flops | bytes accessed | tf_op | source)
XLA Modules:
  0.0 264.5 jit_solution(6659293456052810475)
XLA Ops:
  0.0 1.1 cosine_multiply_fusion
  1.1 7.3 %fusion.2 = f32[1,128,2,64,128]{4,1,3,2,0:T(8,128)S(1)} fusion(bf16[64,128,512]{2,1,0:T(8,128)(2,1)} %param.1, f32[512,1,128]{0,2,1:T(8,128)S(1)} %get-tuple-element.8, f32[512,1,128]{0,2,1:T(8,128)S(1)} %get-tuple-element.7), kind=kOutput, calls=%fused_computation.2 | convolution fusion | flops 6442713088 | bytes 17301504 | tf_op jit(solution)/shard_map/srt,tpb->bpsr/dot_general | solution.py:165
  8.5 4.9 %copy.8 = f32[1,128,2,64,128]{4,3,2,0,1:T(8,128)S(1)} copy(f32[1,128,2,64,128]{4,1,3,2,0:T(8,128)S(1)} %fusion.2) | data formatting | bytes 16777216 | tf_op jit(solution)/shard_map/broadcast_in_dim | solution.py:176
  13.3 109.9 %all_to_all.12 = f32[1,128,2,64,128]{4,3,2,0,1:T(8,128)} all-to-all(f32[1,128,2,64,128]{4,3,2,0,1:T(8,128)S(1)} %copy.8), channel_id=1, replica_groups=mesh['shot'=16,'freq'=8] {'shot','freq'}, dimensions={1} | all-to-all | bytes 16777216 | tf_op jit(solution)/shard_map/all_to_all | solution.py:176
  123.2 18.0 %shard_map.18 = f32[16,8,2,32,128]{4,3,2,1,0:T(8,128)} custom-call(f32[16,8,2,64,128]{4,3,2,1,0:T(8,128)} %bitcast.23), custom_call_target="tpu_custom_call" | custom-call | tf_op jit(solution)/shard_map/pallas_call | solution.py:97
  141.2 5.1 %all-to-all-start.2 = ((f32[1,128,2,32,128]{4,3,2,0,1:T(8,128)}), f32[1,128,2,32,128]{4,3,2,0,1:T(8,128)}, u32[]{:S(2)}, u32[]{:S(2)}) async-start(f32[1,128,2,32,128]{4,3,2,0,1:T(8,128)} %bitcast.26), calls=%async_computation.2 | async-start | bytes 8388608 | tf_op jit(solution)/shard_map/all_to_all | solution.py:184
  146.3 18.1 %shard_map.17 = f32[16,8,2,32,128]{4,3,2,1,0:T(8,128)} custom-call(f32[16,8,2,64,128]{4,3,2,1,0:T(8,128)} %bitcast.24), custom_call_target="tpu_custom_call" | custom-call | tf_op jit(solution)/shard_map/pallas_call | solution.py:97
  164.4 33.5 %all-to-all-done.2 = f32[1,128,2,32,128]{4,3,2,0,1:T(8,128)} async-done(((f32[1,128,2,32,128]{4,3,2,0,1:T(8,128)}), f32[1,128,2,32,128]{4,3,2,0,1:T(8,128)}, u32[]{:S(2)}, u32[]{:S(2)}) %all-to-all-start.2) | async-done | bytes 4194336 | tf_op jit(solution)/shard_map/all_to_all | solution.py:184
  198.0 6.8 %all-to-all-start.1 = ((f32[1,128,2,32,128]{4,3,2,0,1:T(8,128)}), f32[1,128,2,32,128]{4,3,2,0,1:T(8,128)}, u32[]{:S(2)}, u32[]{:S(2)}) async-start(f32[1,128,2,32,128]{4,3,2,0,1:T(8,128)} %bitcast.25), calls=%async_computation.1 | async-start | bytes 8388608 | tf_op jit(solution)/shard_map/all_to_all | solution.py:184
  204.7 1.1 cosine_multiply_fusion.1
  205.9 0.1 maximum_multiply_fusion
  205.9 0.4 copy.7
  206.3 0.4 div.36
  206.7 0.9 fusion.5
  207.6 8.1 %shard_map.19.previous_ref = bf16[64,128,512]{2,1,0:T(8,128)(2,1)} custom-call(bf16[256,512]{1,0:T(8,128)(2,1)} %get-tuple-element.6.w_high, bf16[256,512]{1,0:T(8,128)(2,1)} %get-tuple-element.5.w_low, f32[128,2,32,128]{3,2,1,0:T(8,128)} %bitcast.11.x_ref), custom_call_target="tpu_custom_call" | custom-call | tf_op jit(solution)/shard_map/pallas_call | solution.py:148
  215.6 40.8 %all-to-all-done.1 = f32[1,128,2,32,128]{4,3,2,0,1:T(8,128)} async-done(((f32[1,128,2,32,128]{4,3,2,0,1:T(8,128)}), f32[1,128,2,32,128]{4,3,2,0,1:T(8,128)}, u32[]{:S(2)}, u32[]{:S(2)}) %all-to-all-start.1) | async-done | bytes 4194336 | tf_op jit(solution)/shard_map/all_to_all | solution.py:184
  256.4 8.1 %shard_map.20 = bf16[64,128,512]{2,1,0:T(8,128)(2,1)} custom-call(bf16[256,512]{1,0:T(8,128)(2,1)} %get-tuple-element.6.w_high, bf16[256,512]{1,0:T(8,128)(2,1)} %get-tuple-element.5.w_low, f32[128,2,32,128]{3,2,1,0:T(8,128)} %bitcast.8.x_ref, bf16[64,128,512]{2,1,0:T(8,128)(2,1)} %shard_map.19.previous_ref), custom_call_target="tpu_custom_call", output_to_operand_aliasing={{}: (3, {})} | custom-call | tf_op jit(solution)/shard_map/pallas_call | solution.py:148
  (2 shorter events, 0.0 us)
Async XLA Ops:
  141.2 56.8 %all-to-all-start.2 = ((f32[1,128,2,32,128]{4,3,2,0,1:T(8,128)}), f32[1,128,2,32,128]{4,3,2,0,1:T(8,128)}, u32[]{:S(2)}, u32[]{:S(2)}) async-start(f32[1,128,2,32,128]{4,3,2,0,1:T(8,128)} %bitcast.26), calls=%async_computation.2 | async-start | bytes 8388608 | tf_op jit(solution)/shard_map/all_to_all | solution.py:184
  198.0 58.5 %all-to-all-start.1 = ((f32[1,128,2,32,128]{4,3,2,0,1:T(8,128)}), f32[1,128,2,32,128]{4,3,2,0,1:T(8,128)}, u32[]{:S(2)}, u32[]{:S(2)}) async-start(f32[1,128,2,32,128]{4,3,2,0,1:T(8,128)} %bitcast.25), calls=%async_computation.1 | async-start | bytes 8388608 | tf_op jit(solution)/shard_map/all_to_all | solution.py:184

commit v4 on v3

--- a/solution.py
+++ b/solution.py
@@ -9,7 +9,7 @@
 
 NT = 512
 NF = 128
-PARTS = 2
+SPANS = (24, 40)
 
 
 def make_tables(count_t, count_f):
@@ -39,14 +39,21 @@
     return high.astype(jnp.bfloat16), (x - high).astype(jnp.bfloat16)
 
 
-def square_kernel(n_shot, n_freq, rows, cols, scale, part, y_ref, out_ref, high, low):
+def square_kernel(n_shot, n_freq, rows, cols, scale, first, y_hbm, out_ref, y_ref, sems, high, low):
     width = out_ref.shape[1] * cols
     span = out_ref.shape[3]
     j = pl.program_id(0)
 
+    def copy(a):
+        return pltpu.make_async_copy(y_hbm.at[a], y_ref.at[a], sems.at[a])
+
     @pl.when(j == 0)
     def _():
+        for a in range(n_shot):
+            copy(a).start()
+
         def fill(a, carry):
+            copy(a).wait()
             top = pl.multiple_of(a * rows, rows)
             for b in range(n_freq):
                 real = y_ref[a, b, 0]
@@ -66,7 +73,7 @@
     def product(index):
         def left(ref):
             return jnp.concatenate(
-                [ref[index, pl.ds(a * rows + part * span, span), :] for a in range(n_shot)],
+                [ref[index, pl.ds(a * rows + first, span), :] for a in range(n_shot)],
                 axis=0,
             )
 
@@ -86,23 +93,24 @@
             out_ref[a, b, 1] = imag[tile]
 
 
-def complex_square(blocks, part, parts):
+def complex_square(blocks, first, span):
     n_shot, n_freq, _, rows, cols = blocks.shape
     order = n_shot * rows
-    span = rows // parts
     group = 2
     kernel = functools.partial(
-        square_kernel, n_shot, n_freq, rows, cols, float(-1.0 / (order ** 0.5)), part
+        square_kernel, n_shot, n_freq, rows, cols, float(-1.0 / (order ** 0.5)), first
     )
     return pl.pallas_call(
         kernel,
         out_shape=jax.ShapeDtypeStruct((n_shot, n_freq, 2, span, cols), jnp.float32),
         grid=(n_freq // group,),
-        in_specs=[pl.BlockSpec(memory_space=pltpu.VMEM)],
+        in_specs=[pl.BlockSpec(memory_space=pl.ANY)],
         out_specs=pl.BlockSpec(
             (n_shot, group, 2, span, cols), lambda j: (0, j, 0, 0, 0)
         ),
         scratch_shapes=[
+            pltpu.VMEM(blocks.shape, jnp.float32),
+            pltpu.SemaphoreType.DMA((n_shot,)),
             pltpu.VMEM((3, order, n_freq * cols), jnp.bfloat16),
             pltpu.VMEM((3, order, n_freq * cols), jnp.bfloat16),
         ],
@@ -125,13 +133,13 @@
     out_ref[...] = total.reshape(out_ref.shape).astype(out_ref.dtype)
 
 
-def inverse_transform(home, inverse, part, parts, previous):
+def inverse_transform(home, inverse, first, total, previous):
     n_bins, _, span, cols = home.shape
     steps = inverse.shape[-1]
     table = inverse.reshape(n_bins * 2, steps)
     w_high, w_low = split_outside(table)
     group = 8
-    offset = part * (span // group)
+    offset = first // group
     operands = [w_high, w_low, home]
     in_specs = [
         pl.BlockSpec((n_bins * 2, steps), lambda i: (0, 0)),
@@ -147,7 +155,7 @@
         kernel = functools.partial(inverse_kernel_into, group)
     return pl.pallas_call(
         kernel,
-        out_shape=jax.ShapeDtypeStruct((span * parts, cols, steps), jnp.bfloat16),
+        out_shape=jax.ShapeDtypeStruct((total, cols, steps), jnp.bfloat16),
         grid=(span // group,),
         in_specs=in_specs,
         out_specs=pl.BlockSpec((group, cols, steps), lambda i: (i + offset, 0, 0)),
@@ -178,9 +186,9 @@
     assert local_bins == 1
     blocks = moved.reshape(n_shot, n_freq, 2, rows, cols)
     result = None
-    for part in range(PARTS):
-        pred = complex_square(blocks, part, PARTS)
-        span = pred.shape[3]
+    first = 0
+    for span in SPANS:
+        pred = complex_square(blocks, first, span)
         home = lax.all_to_all(
             pred.reshape(1, n_shot * n_freq, 2, span, cols),
             ("shot", "freq"),
@@ -189,7 +197,9 @@
             tiled=True,
         )
         home = home.reshape(n_shot * n_freq, 2, span, cols)
-        result = inverse_transform(home, inverse, part, PARTS, result)
+        result = inverse_transform(home, inverse, first, rows, result)
+        first += span
+    assert first == rows
     return result
 
 

time: 267 us -> 265 us (level)
  Pallas kernels: 52.2 us -> 47.9 us
    pallas_call x2, Pallas kernels: 36.1 us -> 31.7 us  [complex_square(): pl.pallas_call(kernel, out_shape=jax.ShapeDtypeStruct((n_shot, n_freq, 2,...]
  transfers between devices with their start and end apart: 2 -> 2, of which waited for: 2 -> 2; matrix products, arithmetic and copies ran while one was open for 1% -> 2% of each run, Pallas kernels for 10% -> 9%
where the time goes in v4:
time: 265 us; the launch traced here: 264 us
  blocking collectives  110 us (42%)
  waiting for transfers between devices  74.7 us (28%)
  Pallas kernels  47.9 us (18%)
  starting transfers between devices  11.5 us (4%)
  local copies, waits for them, and re-layouts  8.25 us (3%)
  matrix products  7.32 us (3%)
  other arithmetic  4.2 us (2%)
    all_to_all x1, blocking collectives, per_device(): lax.all_to_all(spectra[None], ('shot', 'freq'), split_axis=1, concat_axis...  110 us
    all_to_all x2, waiting for transfers between devices, per_device(): lax.all_to_all(pred.reshape(1, n_shot * n_freq, 2, span, cols), ('shot',...  74.7 us
    pallas_call x2, Pallas kernels, complex_square(): pl.pallas_call(kernel, out_shape=jax.ShapeDtypeStruct((n_shot, n_freq, 2,...  31.7 us
    pallas_call x2, Pallas kernels, inverse_transform(): pl.pallas_call(kernel, out_shape=jax.ShapeDtypeStruct((total, cols, steps...  16.2 us
    all_to_all x2, starting transfers between devices, per_device(): lax.all_to_all(pred.reshape(1, n_shot * n_freq, 2, span, cols), ('shot',...  11.5 us
    dot_general x1, matrix products, per_device(): jnp.einsum('srt,tpb->bpsr', traces.astype(jnp.float32), forward, precisio...  7.32 us
  transfers between devices with their start and end apart: 2, of which 2 were waited for; matrix products, arithmetic and copies ran while one was open for 2% of the time, Pallas kernels for 9%

profile of v4, /device:TPU:6, one launch (start us, length us, event | category | flops | bytes accessed | tf_op | source)
XLA Modules:
  0.0 263.9 jit_solution(7663876946094245556)
XLA Ops:
  0.0 1.1 cosine_multiply_fusion
  1.1 7.3 %fusion.2 = f32[1,128,2,64,128]{4,1,3,2,0:T(8,128)S(1)} fusion(bf16[64,128,512]{2,1,0:T(8,128)(2,1)} %param.1, f32[512,1,128]{0,2,1:T(8,128)S(1)} %get-tuple-element.8, f32[512,1,128]{0,2,1:T(8,128)S(1)} %get-tuple-element.7), kind=kOutput, calls=%fused_computation.2 | convolution fusion | flops 6442713088 | bytes 17301504 | tf_op jit(solution)/shard_map/srt,tpb->bpsr/dot_general | solution.py:173
  8.5 4.9 %copy.8 = f32[1,128,2,64,128]{4,3,2,0,1:T(8,128)S(1)} copy(f32[1,128,2,64,128]{4,1,3,2,0:T(8,128)S(1)} %fusion.2) | data formatting | bytes 16777216 | tf_op jit(solution)/shard_map/broadcast_in_dim | solution.py:184
  13.3 109.9 %all_to_all.12 = f32[1,128,2,64,128]{4,3,2,0,1:T(8,128)} all-to-all(f32[1,128,2,64,128]{4,3,2,0,1:T(8,128)S(1)} %copy.8), channel_id=1, replica_groups=mesh['shot'=16,'freq'=8] {'shot','freq'}, dimensions={1} | all-to-all | bytes 16777216 | tf_op jit(solution)/shard_map/all_to_all | solution.py:184
  123.2 13.3 %shard_map.18 = f32[16,8,2,24,128]{4,3,2,1,0:T(8,128)} custom-call(f32[16,8,2,64,128]{4,3,2,1,0:T(8,128)} %bitcast.23), custom_call_target="tpu_custom_call" | custom-call | tf_op jit(solution)/shard_map/pallas_call | solution.py:103
  136.5 4.7 %all-to-all-start.2 = ((f32[1,128,2,24,128]{4,3,2,0,1:T(8,128)}), f32[1,128,2,24,128]{4,3,2,0,1:T(8,128)S(1)}, u32[]{:S(2)}, u32[]{:S(2)}) async-start(f32[1,128,2,24,128]{4,3,2,0,1:T(8,128)} %bitcast.27), calls=%async_computation.2 | async-start | bytes 6291456 | tf_op jit(solution)/shard_map/all_to_all | solution.py:192
  141.2 18.4 %shard_map.17 = f32[16,8,2,40,128]{4,3,2,1,0:T(8,128)} custom-call(f32[16,8,2,64,128]{4,3,2,1,0:T(8,128)} %bitcast.24), custom_call_target="tpu_custom_call" | custom-call | tf_op jit(solution)/shard_map/pallas_call | solution.py:103
  159.6 21.3 %all-to-all-done.2 = f32[1,128,2,24,128]{4,3,2,0,1:T(8,128)S(1)} async-done(((f32[1,128,2,24,128]{4,3,2,0,1:T(8,128)}), f32[1,128,2,24,128]{4,3,2,0,1:T(8,128)S(1)}, u32[]{:S(2)}, u32[]{:S(2)}) %all-to-all-start.2) | async-done | bytes 3145760 | tf_op jit(solution)/shard_map/all_to_all | solution.py:192
  180.8 0.0 copy-start
  180.8 6.8 %all-to-all-start.1 = ((f32[1,128,2,40,128]{4,3,2,0,1:T(8,128)}), f32[1,128,2,40,128]{4,3,2,0,1:T(8,128)}, u32[]{:S(2)}, u32[]{:S(2)}) async-start(f32[1,128,2,40,128]{4,3,2,0,1:T(8,128)} %bitcast.25), calls=%async_computation.1 | async-start | bytes 10485760 | tf_op jit(solution)/shard_map/all_to_all | solution.py:192
  187.7 1.1 cosine_multiply_fusion.1
  188.8 0.1 maximum_multiply_fusion
  188.9 1.2 copy.7
  190.1 2.2 div.36
  192.3 1.9 fusion.5
  194.2 0.0 copy-done
  194.2 6.6 %shard_map.19.previous_ref = bf16[64,128,512]{2,1,0:T(8,128)(2,1)} custom-call(bf16[256,512]{1,0:T(8,128)(2,1)} %get-tuple-element.6.w_high, bf16[256,512]{1,0:T(8,128)(2,1)} %get-tuple-element.5.w_low, f32[128,2,24,128]{3,2,1,0:T(8,128)} %bitcast.26), custom_call_target="tpu_custom_call" | custom-call | tf_op jit(solution)/shard_map/pallas_call | solution.py:156
  200.8 53.5 %all-to-all-done.1 = f32[1,128,2,40,128]{4,3,2,0,1:T(8,128)} async-done(((f32[1,128,2,40,128]{4,3,2,0,1:T(8,128)}), f32[1,128,2,40,128]{4,3,2,0,1:T(8,128)}, u32[]{:S(2)}, u32[]{:S(2)}) %all-to-all-start.1) | async-done | bytes 5242912 | tf_op jit(solution)/shard_map/all_to_all | solution.py:192
  254.3 9.6 %shard_map.20 = bf16[64,128,512]{2,1,0:T(8,128)(2,1)} custom-call(bf16[256,512]{1,0:T(8,128)(2,1)} %get-tuple-element.6.w_high, bf16[256,512]{1,0:T(8,128)(2,1)} %get-tuple-element.5.w_low, f32[128,2,40,128]{3,2,1,0:T(8,128)} %bitcast.8.x_ref, bf16[64,128,512]{2,1,0:T(8,128)(2,1)} %shard_map.19.previous_ref), custom_call_target="tpu_custom_call", output_to_operand_aliasing={{}: (3, {})} | custom-call | tf_op jit(solution)/shard_map/pallas_call | solution.py:156
  (2 shorter events, 0.0 us)
Async XLA Ops:
  136.5 44.3 %all-to-all-start.2 = ((f32[1,128,2,24,128]{4,3,2,0,1:T(8,128)}), f32[1,128,2,24,128]{4,3,2,0,1:T(8,128)S(1)}, u32[]{:S(2)}, u32[]{:S(2)}) async-start(f32[1,128,2,24,128]{4,3,2,0,1:T(8,128)} %bitcast.27), calls=%async_computation.2 | async-start | bytes 6291456 | tf_op jit(solution)/shard_map/all_to_all | solution.py:192
  180.8 13.3 %copy-start = (f32[1,128,2,24,128]{4,3,2,0,1:T(8,128)}, f32[1,128,2,24,128]{4,3,2,0,1:T(8,128)S(1)}, u32[]{:S(2)}) copy-start(f32[1,128,2,24,128]{4,3,2,0,1:T(8,128)S(1)} %all-to-all-done.2) | copy-start | bytes 9437188
  180.8 73.4 %all-to-all-start.1 = ((f32[1,128,2,40,128]{4,3,2,0,1:T(8,128)}), f32[1,128,2,40,128]{4,3,2,0,1:T(8,128)}, u32[]{:S(2)}, u32[]{:S(2)}) async-start(f32[1,128,2,40,128]{4,3,2,0,1:T(8,128)} %bitcast.25), calls=%async_computation.1 | async-start | bytes 10485760 | tf_op jit(solution)/shard_map/all_to_all | solution.py:192

commit v5 on v4

--- a/solution.py
+++ b/solution.py
@@ -9,7 +9,7 @@
 
 NT = 512
 NF = 128
-SPANS = (24, 40)
+SPANS = (16, 48)
 
 
 def make_tables(count_t, count_f):

time: 265 us -> 266 us (level)
  waiting for transfers between devices: 74.7 us -> 79.3 us
    all_to_all x2, waiting for transfers between devices: 74.7 us -> 79.3 us  [per_device(): lax.all_to_all(pred.reshape(1, n_shot * n_freq, 2, span, cols), ('shot',...]
  transfers between devices with their start and end apart: 2 -> 2, of which waited for: 2 -> 2; matrix products, arithmetic and copies ran while one was open for 2% -> 1% of each run, Pallas kernels for 9% -> 10%
where the time goes in v5:
time: 266 us; the launch traced here: 265 us
  blocking collectives  110 us (41%)
  waiting for transfers between devices  79.3 us (30%)
  Pallas kernels  47.7 us (18%)
  starting transfers between devices  11.5 us (4%)
  matrix products  7.32 us (3%)
  local copies, waits for them, and re-layouts  5.63 us (2%)
  other arithmetic  3.21 us (1%)
    all_to_all x1, blocking collectives, per_device(): lax.all_to_all(spectra[None], ('shot', 'freq'), split_axis=1, concat_axis...  110 us
    all_to_all x2, waiting for transfers between devices, per_device(): lax.all_to_all(pred.reshape(1, n_shot * n_freq, 2, span, cols), ('shot',...  79.3 us
    pallas_call x2, Pallas kernels, complex_square(): pl.pallas_call(kernel, out_shape=jax.ShapeDtypeStruct((n_shot, n_freq, 2,...  31.6 us
    pallas_call x2, Pallas kernels, inverse_transform(): pl.pallas_call(kernel, out_shape=jax.ShapeDtypeStruct((total, cols, steps...  16.1 us
    all_to_all x2, starting transfers between devices, per_device(): lax.all_to_all(pred.reshape(1, n_shot * n_freq, 2, span, cols), ('shot',...  11.5 us
    dot_general x1, matrix products, per_device(): jnp.einsum('srt,tpb->bpsr', traces.astype(jnp.float32), forward, precisio...  7.32 us
  transfers between devices with their start and end apart: 2, of which 2 were waited for; matrix products, arithmetic and copies ran while one was open for 1% of the time, Pallas kernels for 10%

profile of v5, /device:TPU:6, one launch (start us, length us, event | category | flops | bytes accessed | tf_op | source)
XLA Modules:
  0.0 264.7 jit_solution(4652884454601940624)
XLA Ops:
  0.0 1.1 cosine_multiply_fusion
  1.1 7.3 %fusion.2 = f32[1,128,2,64,128]{4,1,3,2,0:T(8,128)S(1)} fusion(bf16[64,128,512]{2,1,0:T(8,128)(2,1)} %param.1, f32[512,1,128]{0,2,1:T(8,128)S(1)} %get-tuple-element.8, f32[512,1,128]{0,2,1:T(8,128)S(1)} %get-tuple-element.7), kind=kOutput, calls=%fused_computation.2 | convolution fusion | flops 6442713088 | bytes 17301504 | tf_op jit(solution)/shard_map/srt,tpb->bpsr/dot_general | solution.py:173
  8.5 4.9 %copy.8 = f32[1,128,2,64,128]{4,3,2,0,1:T(8,128)S(1)} copy(f32[1,128,2,64,128]{4,1,3,2,0:T(8,128)S(1)} %fusion.2) | data formatting | bytes 16777216 | tf_op jit(solution)/shard_map/broadcast_in_dim | solution.py:184
  13.3 109.9 %all_to_all.12 = f32[1,128,2,64,128]{4,3,2,0,1:T(8,128)} all-to-all(f32[1,128,2,64,128]{4,3,2,0,1:T(8,128)S(1)} %copy.8), channel_id=1, replica_groups=mesh['shot'=16,'freq'=8] {'shot','freq'}, dimensions={1} | all-to-all | bytes 16777216 | tf_op jit(solution)/shard_map/all_to_all | solution.py:184
  123.2 10.8 %shard_map.18 = f32[16,8,2,16,128]{4,3,2,1,0:T(8,128)} custom-call(f32[16,8,2,64,128]{4,3,2,1,0:T(8,128)} %bitcast.23), custom_call_target="tpu_custom_call" | custom-call | tf_op jit(solution)/shard_map/pallas_call | solution.py:103
  134.0 4.7 %all-to-all-start.2 = ((f32[1,128,2,16,128]{4,3,2,0,1:T(8,128)}), f32[1,128,2,16,128]{4,3,2,0,1:T(8,128)S(1)}, u32[]{:S(2)}, u32[]{:S(2)}) async-start(f32[1,128,2,16,128]{4,3,2,0,1:T(8,128)} %bitcast.26), calls=%async_computation.2 | async-start | bytes 4194304 | tf_op jit(solution)/shard_map/all_to_all | solution.py:192
  138.7 20.8 %shard_map.17 = f32[16,8,2,48,128]{4,3,2,1,0:T(8,128)} custom-call(f32[16,8,2,64,128]{4,3,2,1,0:T(8,128)} %bitcast.24), custom_call_target="tpu_custom_call" | custom-call | tf_op jit(solution)/shard_map/pallas_call | solution.py:103
  159.6 7.6 %all-to-all-done.2 = f32[1,128,2,16,128]{4,3,2,0,1:T(8,128)S(1)} async-done(((f32[1,128,2,16,128]{4,3,2,0,1:T(8,128)}), f32[1,128,2,16,128]{4,3,2,0,1:T(8,128)S(1)}, u32[]{:S(2)}, u32[]{:S(2)}) %all-to-all-start.2) | async-done | bytes 2097184 | tf_op jit(solution)/shard_map/all_to_all | solution.py:192
  167.2 0.0 copy-start
  167.2 6.9 %all-to-all-start.1 = ((f32[1,128,2,48,128]{4,3,2,0,1:T(8,128)}), f32[1,128,2,48,128]{4,3,2,0,1:T(8,128)}, u32[]{:S(2)}, u32[]{:S(2)}) async-start(f32[1,128,2,48,128]{4,3,2,0,1:T(8,128)} %bitcast.25), calls=%async_computation.1 | async-start | bytes 12582912 | tf_op jit(solution)/shard_map/all_to_all | solution.py:192
  174.1 1.1 cosine_multiply_fusion.1
  175.2 0.1 maximum_multiply_fusion
  175.3 0.4 copy.7
  175.7 0.4 div.36
  176.0 0.9 fusion.5
  176.9 0.0 copy-done
  176.9 5.0 %shard_map.19.previous_ref = bf16[64,128,512]{2,1,0:T(8,128)(2,1)} custom-call(bf16[256,512]{1,0:T(8,128)(2,1)} %get-tuple-element.6.w_high, bf16[256,512]{1,0:T(8,128)(2,1)} %get-tuple-element.5.w_low, f32[128,2,16,128]{3,2,1,0:T(8,128)} %bitcast.27), custom_call_target="tpu_custom_call" | custom-call | tf_op jit(solution)/shard_map/pallas_call | solution.py:156
  182.0 71.7 %all-to-all-done.1 = f32[1,128,2,48,128]{4,3,2,0,1:T(8,128)} async-done(((f32[1,128,2,48,128]{4,3,2,0,1:T(8,128)}), f32[1,128,2,48,128]{4,3,2,0,1:T(8,128)}, u32[]{:S(2)}, u32[]{:S(2)}) %all-to-all-start.1) | async-done | bytes 6291488 | tf_op jit(solution)/shard_map/all_to_all | solution.py:192
  253.6 11.1 %shard_map.20 = bf16[64,128,512]{2,1,0:T(8,128)(2,1)} custom-call(bf16[256,512]{1,0:T(8,128)(2,1)} %get-tuple-element.6.w_high, bf16[256,512]{1,0:T(8,128)(2,1)} %get-tuple-element.5.w_low, f32[128,2,48,128]{3,2,1,0:T(8,128)} %bitcast.8.x_ref, bf16[64,128,512]{2,1,0:T(8,128)(2,1)} %shard_map.19.previous_ref), custom_call_target="tpu_custom_call", output_to_operand_aliasing={{}: (3, {})} | custom-call | tf_op jit(solution)/shard_map/pallas_call | solution.py:156
  (2 shorter events, 0.0 us)
Async XLA Ops:
  134.0 33.2 %all-to-all-start.2 = ((f32[1,128,2,16,128]{4,3,2,0,1:T(8,128)}), f32[1,128,2,16,128]{4,3,2,0,1:T(8,128)S(1)}, u32[]{:S(2)}, u32[]{:S(2)}) async-start(f32[1,128,2,16,128]{4,3,2,0,1:T(8,128)} %bitcast.26), calls=%async_computation.2 | async-start | bytes 4194304 | tf_op jit(solution)/shard_map/all_to_all | solution.py:192
  167.2 9.7 %copy-start = (f32[1,128,2,16,128]{4,3,2,0,1:T(8,128)}, f32[1,128,2,16,128]{4,3,2,0,1:T(8,128)S(1)}, u32[]{:S(2)}) copy-start(f32[1,128,2,16,128]{4,3,2,0,1:T(8,128)S(1)} %all-to-all-done.2) | copy-start | bytes 6291460
  167.2 86.4 %all-to-all-start.1 = ((f32[1,128,2,48,128]{4,3,2,0,1:T(8,128)}), f32[1,128,2,48,128]{4,3,2,0,1:T(8,128)}, u32[]{:S(2)}, u32[]{:S(2)}) async-start(f32[1,128,2,48,128]{4,3,2,0,1:T(8,128)} %bitcast.25), calls=%async_computation.1 | async-start | bytes 12582912 | tf_op jit(solution)/shard_map/all_to_all | solution.py:192

commit v6 on v4

--- a/solution.py
+++ b/solution.py
@@ -122,11 +122,8 @@
 
 def inverse_kernel(group, w_high, w_low, x_ref, out_ref):
     n_bins, parts, _, cols = x_ref.shape
-    pieces = []
-    for s in range(group):
-        piece = x_ref[:, :, s, :].reshape(n_bins * parts, cols)
-        pieces.append(piece.T)
-    stacked = jnp.concatenate(pieces, axis=0)
+    block = x_ref[...].reshape(n_bins * parts, group, cols)
+    stacked = pltpu.einshape("ksr->(sr)k", block)
     high, low = split(stacked)
     dot = functools.partial(jnp.dot, preferred_element_type=jnp.float32)
     total = dot(high, w_high[...]) + dot(high, w_low[...]) + dot(low, w_high[...])
@@ -170,12 +167,10 @@
 
 def per_device(traces):
     forward, inverse = make_tables(NT, NF)
-    spectra = jnp.einsum(
-        "srt,tpb->bpsr",
-        traces.astype(jnp.float32),
-        forward,
-        precision=lax.Precision.HIGH,
-        preferred_element_type=jnp.float32,
+    f_high, f_low = split_outside(forward)
+    spectra = sum(
+        jnp.einsum("srt,tpb->bpsr", traces, half, preferred_element_type=jnp.float32)
+        for half in (f_high, f_low)
     )
     rows = traces.shape[0]
     cols = traces.shape[1]

time: 265 us -> 278 us (1.049)
  matrix products: 7.32 us -> 18.1 us
  local copies, waits for them, and re-layouts: 8.25 us -> 11.7 us
    dot_general x1 -> x2, matrix products: 7.32 us -> 18.1 us  [per_device(): jnp.einsum('srt,tpb->bpsr', traces, half, preferred_element_type=jnp.floa...]
    broadcast_in_dim x1, local copies, waits for them, and re-layouts: 4.86 us -> 8.24 us  [per_device(): spectra[None]]
where the time goes in v6:
time: 278 us; the launch traced here: 277 us
  blocking collectives  110 us (40%)
  waiting for transfers between devices  75.2 us (27%)
  Pallas kernels  46.7 us (17%)
  matrix products  18.1 us (7%)
  local copies, waits for them, and re-layouts  11.7 us (4%)
  starting transfers between devices  11.5 us (4%)
  other arithmetic  4.19 us (2%)
    all_to_all x1, blocking collectives, per_device(): lax.all_to_all(spectra[None], ('shot', 'freq'), split_axis=1, concat_axis...  110 us
    all_to_all x2, waiting for transfers between devices, per_device(): lax.all_to_all(pred.reshape(1, n_shot * n_freq, 2, span, cols), ('shot',...  75.2 us
    pallas_call x2, Pallas kernels, complex_square(): pl.pallas_call(kernel, out_shape=jax.ShapeDtypeStruct((n_shot, n_freq, 2,...  31.6 us
    dot_general x2, matrix products, per_device(): jnp.einsum('srt,tpb->bpsr', traces, half, preferred_element_type=jnp.floa...  18.1 us
    pallas_call x2, Pallas kernels, inverse_transform(): pl.pallas_call(kernel, out_shape=jax.ShapeDtypeStruct((total, cols, steps...  15.1 us
    all_to_all x2, starting transfers between devices, per_device(): lax.all_to_all(pred.reshape(1, n_shot * n_freq, 2, span, cols), ('shot',...  11.5 us
    broadcast_in_dim x1, local copies, waits for them, and re-layouts, per_device(): spectra[None]  8.24 us
  transfers between devices with their start and end apart: 2, of which 2 were waited for; matrix products, arithmetic and copies ran while one was open for 2% of the time, Pallas kernels for 9%

profile of v6, /device:TPU:6, one launch (start us, length us, event | category | flops | bytes accessed | tf_op | source)
XLA Modules:
  0.0 277.3 jit_solution(12674505552075277291)
XLA Ops:
  0.0 1.1 cosine_multiply_fusion
  1.1 0.0 slice-start
  1.1 0.0 slice-start.1
  1.2 11.2 %fusion = f32[2,128,64,128]{3,1,2,0:T(8,128)} fusion(bf16[64,128,512]{2,1,0:T(8,128)(2,1)} %param.1, f32[512,1,128]{0,2,1:T(8,128)S(1)} %get-tuple-element.8, f32[512,1,128]{0,2,1:T(8,128)S(1)} %get-tuple-element.7), kind=kOutput, calls=%fused_computation | convolution fusion | flops 2148139008 | bytes 17301504 | tf_op jit(solution)/shard_map/srt,tpb->bpsr/dot_general | solution.py:172
  12.4 0.0 slice-done
  12.4 0.0 slice-done.1
  12.4 6.9 %add_bitcast_fusion = f32[1,128,2,64,128]{4,1,3,2,0:T(8,128)} fusion(f32[2,128,64,128]{3,1,2,0:T(8,128)} %fusion, bf16[64,128,512]{2,1,0:T(8,128)(2,1)S(1)} %bitcast.31, f32[512,1,128]{0,2,1:T(8,128)S(1)} %get-tuple-element.8, f32[512,1,128]{0,2,1:T(8,128)S(1)} %get-tuple-element.7), kind=kOutput, calls=%fused_computation.4 | convolution fusion | flops 2150105088 | bytes 25690112 | tf_op jit(solution)/shard_map/srt,tpb->bpsr/dot_general | solution.py:172
  19.3 8.2 %copy.8 = f32[1,128,2,64,128]{4,3,2,0,1:T(8,128)S(1)} copy(f32[1,128,2,64,128]{4,1,3,2,0:T(8,128)} %add_bitcast_fusion) | data formatting | bytes 16777216 | tf_op jit(solution)/shard_map/broadcast_in_dim | solution.py:179
  27.5 109.9 %all_to_all.12 = f32[1,128,2,64,128]{4,3,2,0,1:T(8,128)} all-to-all(f32[1,128,2,64,128]{4,3,2,0,1:T(8,128)S(1)} %copy.8), channel_id=1, replica_groups=mesh['shot'=16,'freq'=8] {'shot','freq'}, dimensions={1} | all-to-all | bytes 16777216 | tf_op jit(solution)/shard_map/all_to_all | solution.py:179
  137.4 13.3 %shard_map.18 = f32[16,8,2,24,128]{4,3,2,1,0:T(8,128)} custom-call(f32[16,8,2,64,128]{4,3,2,1,0:T(8,128)} %bitcast.32), custom_call_target="tpu_custom_call" | custom-call | tf_op jit(solution)/shard_map/pallas_call | solution.py:103
  150.7 4.7 %all-to-all-start.2 = ((f32[1,128,2,24,128]{4,3,2,0,1:T(8,128)}), f32[1,128,2,24,128]{4,3,2,0,1:T(8,128)S(1)}, u32[]{:S(2)}, u32[]{:S(2)}) async-start(f32[1,128,2,24,128]{4,3,2,0,1:T(8,128)} %bitcast.36), calls=%async_computation.2 | async-start | bytes 6291456 | tf_op jit(solution)/shard_map/all_to_all | solution.py:187
  155.4 18.3 %shard_map.17 = f32[16,8,2,40,128]{4,3,2,1,0:T(8,128)} custom-call(f32[16,8,2,64,128]{4,3,2,1,0:T(8,128)} %bitcast.33), custom_call_target="tpu_custom_call" | custom-call | tf_op jit(solution)/shard_map/pallas_call | solution.py:103
  173.7 21.3 %all-to-all-done.2 = f32[1,128,2,24,128]{4,3,2,0,1:T(8,128)S(1)} async-done(((f32[1,128,2,24,128]{4,3,2,0,1:T(8,128)}), f32[1,128,2,24,128]{4,3,2,0,1:T(8,128)S(1)}, u32[]{:S(2)}, u32[]{:S(2)}) %all-to-all-start.2) | async-done | bytes 3145760 | tf_op jit(solution)/shard_map/all_to_all | solution.py:187
  195.0 0.0 copy-start
  195.0 6.8 %all-to-all-start.1 = ((f32[1,128,2,40,128]{4,3,2,0,1:T(8,128)}), f32[1,128,2,40,128]{4,3,2,0,1:T(8,128)}, u32[]{:S(2)}, u32[]{:S(2)}) async-start(f32[1,128,2,40,128]{4,3,2,0,1:T(8,128)} %bitcast.34), calls=%async_computation.1 | async-start | bytes 10485760 | tf_op jit(solution)/shard_map/all_to_all | solution.py:187
  201.8 1.1 cosine_multiply_fusion.1
  203.0 0.1 maximum_multiply_fusion
  203.0 1.2 copy.7
  204.2 2.2 div.36
  206.4 1.9 fusion.6
  208.3 0.0 copy-done
  208.3 6.2 %shard_map.19.previous_ref = bf16[64,128,512]{2,1,0:T(8,128)(2,1)} custom-call(bf16[256,512]{1,0:T(8,128)(2,1)} %get-tuple-element.6.w_high, bf16[256,512]{1,0:T(8,128)(2,1)} %get-tuple-element.5.w_low, f32[128,2,24,128]{3,2,1,0:T(8,128)} %bitcast.35), custom_call_target="tpu_custom_call" | custom-call | tf_op jit(solution)/shard_map/pallas_call | solution.py:153
  214.5 53.9 %all-to-all-done.1 = f32[1,128,2,40,128]{4,3,2,0,1:T(8,128)} async-done(((f32[1,128,2,40,128]{4,3,2,0,1:T(8,128)}), f32[1,128,2,40,128]{4,3,2,0,1:T(8,128)}, u32[]{:S(2)}, u32[]{:S(2)}) %all-to-all-start.1) | async-done | bytes 5242912 | tf_op jit(solution)/shard_map/all_to_all | solution.py:187
  268.4 8.9 %shard_map.20 = bf16[64,128,512]{2,1,0:T(8,128)(2,1)} custom-call(bf16[256,512]{1,0:T(8,128)(2,1)} %get-tuple-element.6.w_high, bf16[256,512]{1,0:T(8,128)(2,1)} %get-tuple-element.5.w_low, f32[128,2,40,128]{3,2,1,0:T(8,128)} %bitcast.10.x_ref, bf16[64,128,512]{2,1,0:T(8,128)(2,1)} %shard_map.19.previous_ref), custom_call_target="tpu_custom_call", output_to_operand_aliasing={{}: (3, {})} | custom-call | tf_op jit(solution)/shard_map/pallas_call | solution.py:153
  (3 shorter events, 0.0 us)
Async XLA Ops:
  1.1 11.2 %slice-start = ((s8[8388608]{0:T(1024)(128)(4,1)}), s8[4194304]{0:T(1024)(128)(4,1)S(1)}, s32[]{:S(2)}) async-start(s8[8388608]{0:T(1024)(128)(4,1)} %bitcast.30), calls=%async_computation.3 | async-start | bytes 8388608
  1.1 11.2 %slice-start.1 = ((s8[8388608]{0:T(1024)(128)(4,1)}), s8[4194304]{0:T(1024)(128)(4,1)S(1)}, s32[]{:S(2)}) async-start(s8[8388608]{0:T(1024)(128)(4,1)} %bitcast.30), calls=%async_computation.4 | async-start | bytes 8388608
  150.7 44.3 %all-to-all-start.2 = ((f32[1,128,2,24,128]{4,3,2,0,1:T(8,128)}), f32[1,128,2,24,128]{4,3,2,0,1:T(8,128)S(1)}, u32[]{:S(2)}, u32[]{:S(2)}) async-start(f32[1,128,2,24,128]{4,3,2,0,1:T(8,128)} %bitcast.36), calls=%async_computation.2 | async-start | bytes 6291456 | tf_op jit(solution)/shard_map/all_to_all | solution.py:187
  195.0 13.3 %copy-start = (f32[1,128,2,24,128]{4,3,2,0,1:T(8,128)}, f32[1,128,2,24,128]{4,3,2,0,1:T(8,128)S(1)}, u32[]{:S(2)}) copy-start(f32[1,128,2,24,128]{4,3,2,0,1:T(8,128)S(1)} %all-to-all-done.2) | copy-start | bytes 9437188
  195.0 73.4 %all-to-all-start.1 = ((f32[1,128,2,40,128]{4,3,2,0,1:T(8,128)}), f32[1,128,2,40,128]{4,3,2,0,1:T(8,128)}, u32[]{:S(2)}, u32[]{:S(2)}) async-start(f32[1,128,2,40,128]{4,3,2,0,1:T(8,128)} %bitcast.34), calls=%async_computation.1 | async-start | bytes 10485760 | tf_op jit(solution)/shard_map/all_to_all | solution.py:187

commit v7 on v4

--- a/solution.py
+++ b/solution.py
@@ -122,11 +122,8 @@
 
 def inverse_kernel(group, w_high, w_low, x_ref, out_ref):
     n_bins, parts, _, cols = x_ref.shape
-    pieces = []
-    for s in range(group):
-        piece = x_ref[:, :, s, :].reshape(n_bins * parts, cols)
-        pieces.append(piece.T)
-    stacked = jnp.concatenate(pieces, axis=0)
+    block = x_ref[...].reshape(n_bins * parts, group, cols)
+    stacked = pltpu.einshape("ksr->(sr)k", block)
     high, low = split(stacked)
     dot = functools.partial(jnp.dot, preferred_element_type=jnp.float32)
     total = dot(high, w_high[...]) + dot(high, w_low[...]) + dot(low, w_high[...])

time: 265 us -> 264 us (level)
  no operation moved by 1% of the time
where the time goes in v7:
time: 264 us; the launch traced here: 263 us
  blocking collectives  110 us (42%)
  waiting for transfers between devices  75.2 us (28%)
  Pallas kernels  46.7 us (18%)
  starting transfers between devices  11.5 us (4%)
  local copies, waits for them, and re-layouts  8.25 us (3%)
  matrix products  7.32 us (3%)
  other arithmetic  4.2 us (2%)
    all_to_all x1, blocking collectives, per_device(): lax.all_to_all(spectra[None], ('shot', 'freq'), split_axis=1, concat_axis...  110 us
    all_to_all x2, waiting for transfers between devices, per_device(): lax.all_to_all(pred.reshape(1, n_shot * n_freq, 2, span, cols), ('shot',...  75.2 us
    pallas_call x2, Pallas kernels, complex_square(): pl.pallas_call(kernel, out_shape=jax.ShapeDtypeStruct((n_shot, n_freq, 2,...  31.7 us
    pallas_call x2, Pallas kernels, inverse_transform(): pl.pallas_call(kernel, out_shape=jax.ShapeDtypeStruct((total, cols, steps...  15.1 us
    all_to_all x2, starting transfers between devices, per_device(): lax.all_to_all(pred.reshape(1, n_shot * n_freq, 2, span, cols), ('shot',...  11.5 us
    dot_general x1, matrix products, per_device(): jnp.einsum('srt,tpb->bpsr', traces.astype(jnp.float32), forward, precisio...  7.32 us
  transfers between devices with their start and end apart: 2, of which 2 were waited for; matrix products, arithmetic and copies ran while one was open for 2% of the time, Pallas kernels for 9%

profile of v7, /device:TPU:6, one launch (start us, length us, event | category | flops | bytes accessed | tf_op | source)
XLA Modules:
  0.0 263.2 jit_solution(14434557307887297423)
XLA Ops:
  0.0 1.1 cosine_multiply_fusion
  1.1 7.3 %fusion.2 = f32[1,128,2,64,128]{4,1,3,2,0:T(8,128)S(1)} fusion(bf16[64,128,512]{2,1,0:T(8,128)(2,1)} %param.1, f32[512,1,128]{0,2,1:T(8,128)S(1)} %get-tuple-element.8, f32[512,1,128]{0,2,1:T(8,128)S(1)} %get-tuple-element.7), kind=kOutput, calls=%fused_computation.2 | convolution fusion | flops 6442713088 | bytes 17301504 | tf_op jit(solution)/shard_map/srt,tpb->bpsr/dot_general | solution.py:170
  8.5 4.9 %copy.8 = f32[1,128,2,64,128]{4,3,2,0,1:T(8,128)S(1)} copy(f32[1,128,2,64,128]{4,1,3,2,0:T(8,128)S(1)} %fusion.2) | data formatting | bytes 16777216 | tf_op jit(solution)/shard_map/broadcast_in_dim | solution.py:181
  13.3 109.9 %all_to_all.12 = f32[1,128,2,64,128]{4,3,2,0,1:T(8,128)} all-to-all(f32[1,128,2,64,128]{4,3,2,0,1:T(8,128)S(1)} %copy.8), channel_id=1, replica_groups=mesh['shot'=16,'freq'=8] {'shot','freq'}, dimensions={1} | all-to-all | bytes 16777216 | tf_op jit(solution)/shard_map/all_to_all | solution.py:181
  123.2 13.3 %shard_map.18 = f32[16,8,2,24,128]{4,3,2,1,0:T(8,128)} custom-call(f32[16,8,2,64,128]{4,3,2,1,0:T(8,128)} %bitcast.23), custom_call_target="tpu_custom_call" | custom-call | tf_op jit(solution)/shard_map/pallas_call | solution.py:103
  136.5 4.7 %all-to-all-start.2 = ((f32[1,128,2,24,128]{4,3,2,0,1:T(8,128)}), f32[1,128,2,24,128]{4,3,2,0,1:T(8,128)S(1)}, u32[]{:S(2)}, u32[]{:S(2)}) async-start(f32[1,128,2,24,128]{4,3,2,0,1:T(8,128)} %bitcast.27), calls=%async_computation.2 | async-start | bytes 6291456 | tf_op jit(solution)/shard_map/all_to_all | solution.py:189
  141.2 18.4 %shard_map.17 = f32[16,8,2,40,128]{4,3,2,1,0:T(8,128)} custom-call(f32[16,8,2,64,128]{4,3,2,1,0:T(8,128)} %bitcast.24), custom_call_target="tpu_custom_call" | custom-call | tf_op jit(solution)/shard_map/pallas_call | solution.py:103
  159.6 21.3 %all-to-all-done.2 = f32[1,128,2,24,128]{4,3,2,0,1:T(8,128)S(1)} async-done(((f32[1,128,2,24,128]{4,3,2,0,1:T(8,128)}), f32[1,128,2,24,128]{4,3,2,0,1:T(8,128)S(1)}, u32[]{:S(2)}, u32[]{:S(2)}) %all-to-all-start.2) | async-done | bytes 3145760 | tf_op jit(solution)/shard_map/all_to_all | solution.py:189
  180.8 0.0 copy-start
  180.8 6.8 %all-to-all-start.1 = ((f32[1,128,2,40,128]{4,3,2,0,1:T(8,128)}), f32[1,128,2,40,128]{4,3,2,0,1:T(8,128)}, u32[]{:S(2)}, u32[]{:S(2)}) async-start(f32[1,128,2,40,128]{4,3,2,0,1:T(8,128)} %bitcast.25), calls=%async_computation.1 | async-start | bytes 10485760 | tf_op jit(solution)/shard_map/all_to_all | solution.py:189
  187.7 1.1 cosine_multiply_fusion.1
  188.8 0.1 maximum_multiply_fusion
  188.9 1.2 copy.7
  190.1 2.2 div.36
  192.3 1.9 fusion.5
  194.2 0.0 copy-done
  194.2 6.2 %shard_map.19.previous_ref = bf16[64,128,512]{2,1,0:T(8,128)(2,1)} custom-call(bf16[256,512]{1,0:T(8,128)(2,1)} %get-tuple-element.6.w_high, bf16[256,512]{1,0:T(8,128)(2,1)} %get-tuple-element.5.w_low, f32[128,2,24,128]{3,2,1,0:T(8,128)} %bitcast.26), custom_call_target="tpu_custom_call" | custom-call | tf_op jit(solution)/shard_map/pallas_call | solution.py:153
  200.3 54.0 %all-to-all-done.1 = f32[1,128,2,40,128]{4,3,2,0,1:T(8,128)} async-done(((f32[1,128,2,40,128]{4,3,2,0,1:T(8,128)}), f32[1,128,2,40,128]{4,3,2,0,1:T(8,128)}, u32[]{:S(2)}, u32[]{:S(2)}) %all-to-all-start.1) | async-done | bytes 5242912 | tf_op jit(solution)/shard_map/all_to_all | solution.py:189
  254.3 8.9 %shard_map.20 = bf16[64,128,512]{2,1,0:T(8,128)(2,1)} custom-call(bf16[256,512]{1,0:T(8,128)(2,1)} %get-tuple-element.6.w_high, bf16[256,512]{1,0:T(8,128)(2,1)} %get-tuple-element.5.w_low, f32[128,2,40,128]{3,2,1,0:T(8,128)} %bitcast.8.x_ref, bf16[64,128,512]{2,1,0:T(8,128)(2,1)} %shard_map.19.previous_ref), custom_call_target="tpu_custom_call", output_to_operand_aliasing={{}: (3, {})} | custom-call | tf_op jit(solution)/shard_map/pallas_call | solution.py:153
  (2 shorter events, 0.0 us)
Async XLA Ops:
  136.5 44.3 %all-to-all-start.2 = ((f32[1,128,2,24,128]{4,3,2,0,1:T(8,128)}), f32[1,128,2,24,128]{4,3,2,0,1:T(8,128)S(1)}, u32[]{:S(2)}, u32[]{:S(2)}) async-start(f32[1,128,2,24,128]{4,3,2,0,1:T(8,128)} %bitcast.27), calls=%async_computation.2 | async-start | bytes 6291456 | tf_op jit(solution)/shard_map/all_to_all | solution.py:189
  180.8 13.3 %copy-start = (f32[1,128,2,24,128]{4,3,2,0,1:T(8,128)}, f32[1,128,2,24,128]{4,3,2,0,1:T(8,128)S(1)}, u32[]{:S(2)}) copy-start(f32[1,128,2,24,128]{4,3,2,0,1:T(8,128)S(1)} %all-to-all-done.2) | copy-start | bytes 9437188
  180.8 73.4 %all-to-all-start.1 = ((f32[1,128,2,40,128]{4,3,2,0,1:T(8,128)}), f32[1,128,2,40,128]{4,3,2,0,1:T(8,128)}, u32[]{:S(2)}, u32[]{:S(2)}) async-start(f32[1,128,2,40,128]{4,3,2,0,1:T(8,128)} %bitcast.25), calls=%async_computation.1 | async-start | bytes 10485760 | tf_op jit(solution)/shard_map/all_to_all | solution.py:189

commit v8 on v7

--- a/solution.py
+++ b/solution.py
@@ -166,7 +166,9 @@
 
 
 def per_device(traces):
-    forward, inverse = make_tables(NT, NF)
+    _, inverse = make_tables(NT, NF)
+    with jax.ensure_compile_time_eval():
+        forward = make_tables(NT, NF)[0]
     spectra = jnp.einsum(
         "srt,tpb->bpsr",
         traces.astype(jnp.float32),

time: 264 us -> 263 us (level)
  no operation moved by 1% of the time
where the time goes in v8:
time: 263 us; the launch traced here: 262 us
  blocking collectives  110 us (42%)
  waiting for transfers between devices  75.2 us (29%)
  Pallas kernels  46.7 us (18%)
  starting transfers between devices  11.5 us (4%)
  local copies, waits for them, and re-layouts  8.25 us (3%)
  matrix products  7.4 us (3%)
  other arithmetic  3.07 us (1%)
    all_to_all x1, blocking collectives, per_device(): lax.all_to_all(spectra[None], ('shot', 'freq'), split_axis=1, concat_axis...  110 us
    all_to_all x2, waiting for transfers between devices, per_device(): lax.all_to_all(pred.reshape(1, n_shot * n_freq, 2, span, cols), ('shot',...  75.2 us
    pallas_call x2, Pallas kernels, complex_square(): pl.pallas_call(kernel, out_shape=jax.ShapeDtypeStruct((n_shot, n_freq, 2,...  31.6 us
    pallas_call x2, Pallas kernels, inverse_transform(): pl.pallas_call(kernel, out_shape=jax.ShapeDtypeStruct((total, cols, steps...  15.1 us
    all_to_all x2, starting transfers between devices, per_device(): lax.all_to_all(pred.reshape(1, n_shot * n_freq, 2, span, cols), ('shot',...  11.5 us
    dot_general x1, matrix products, per_device(): jnp.einsum('srt,tpb->bpsr', traces.astype(jnp.float32), forward, precisio...  7.4 us
  transfers between devices with their start and end apart: 2, of which 2 were waited for; matrix products, arithmetic and copies ran while one was open for 2% of the time, Pallas kernels for 9%

profile of v8, /device:TPU:6, one launch (start us, length us, event | category | flops | bytes accessed | tf_op | source)
XLA Modules:
  0.0 262.1 jit_solution(244021461540308898)
XLA Ops:
  0.0 7.4 %fusion.2 = f32[1,128,2,64,128]{4,1,3,2,0:T(8,128)S(1)} fusion(f32[512,2,128,1]{0,2,3,1:T(8,128)} %constant.37, bf16[64,128,512]{2,1,0:T(8,128)(2,1)} %param.2), kind=kOutput, calls=%fused_computation.2 | convolution fusion | flops 6442450944 | bytes 17301504 | tf_op jit(solution)/shard_map/srt,tpb->bpsr/dot_general | solution.py:172
  7.4 4.9 %copy.9 = f32[1,128,2,64,128]{4,3,2,0,1:T(8,128)S(1)} copy(f32[1,128,2,64,128]{4,1,3,2,0:T(8,128)S(1)} %fusion.2) | data formatting | bytes 16777216 | tf_op jit(solution)/shard_map/broadcast_in_dim | solution.py:183
  12.3 109.9 %all_to_all.12 = f32[1,128,2,64,128]{4,3,2,0,1:T(8,128)} all-to-all(f32[1,128,2,64,128]{4,3,2,0,1:T(8,128)S(1)} %copy.9), channel_id=1, replica_groups=mesh['shot'=16,'freq'=8] {'shot','freq'}, dimensions={1} | all-to-all | bytes 16777216 | tf_op jit(solution)/shard_map/all_to_all | solution.py:183
  122.1 13.3 %shard_map.29 = f32[16,8,2,24,128]{4,3,2,1,0:T(8,128)} custom-call(f32[16,8,2,64,128]{4,3,2,1,0:T(8,128)} %bitcast.22), custom_call_target="tpu_custom_call" | custom-call | tf_op jit(solution)/shard_map/pallas_call | solution.py:103
  135.5 4.7 %all-to-all-start.2 = ((f32[1,128,2,24,128]{4,3,2,0,1:T(8,128)}), f32[1,128,2,24,128]{4,3,2,0,1:T(8,128)S(1)}, u32[]{:S(2)}, u32[]{:S(2)}) async-start(f32[1,128,2,24,128]{4,3,2,0,1:T(8,128)} %bitcast.26), calls=%async_computation.2 | async-start | bytes 6291456 | tf_op jit(solution)/shard_map/all_to_all | solution.py:191
  140.2 18.3 %shard_map.28 = f32[16,8,2,40,128]{4,3,2,1,0:T(8,128)} custom-call(f32[16,8,2,64,128]{4,3,2,1,0:T(8,128)} %bitcast.23), custom_call_target="tpu_custom_call" | custom-call | tf_op jit(solution)/shard_map/pallas_call | solution.py:103
  158.5 21.3 %all-to-all-done.2 = f32[1,128,2,24,128]{4,3,2,0,1:T(8,128)S(1)} async-done(((f32[1,128,2,24,128]{4,3,2,0,1:T(8,128)}), f32[1,128,2,24,128]{4,3,2,0,1:T(8,128)S(1)}, u32[]{:S(2)}, u32[]{:S(2)}) %all-to-all-start.2) | async-done | bytes 3145760 | tf_op jit(solution)/shard_map/all_to_all | solution.py:191
  179.8 0.0 copy-start
  179.8 6.8 %all-to-all-start.1 = ((f32[1,128,2,40,128]{4,3,2,0,1:T(8,128)}), f32[1,128,2,40,128]{4,3,2,0,1:T(8,128)}, u32[]{:S(2)}, u32[]{:S(2)}) async-start(f32[1,128,2,40,128]{4,3,2,0,1:T(8,128)} %bitcast.24), calls=%async_computation.1 | async-start | bytes 10485760 | tf_op jit(solution)/shard_map/all_to_all | solution.py:191
  186.7 1.1 cosine_multiply_fusion
  187.8 0.1 maximum_multiply_fusion
  187.8 1.2 copy.8
  189.0 2.2 div.22
  191.2 1.9 fusion.5
  193.1 0.0 copy-done
  193.1 6.2 %shard_map.30.previous_ref = bf16[64,128,512]{2,1,0:T(8,128)(2,1)} custom-call(bf16[256,512]{1,0:T(8,128)(2,1)} %get-tuple-element.6.w_high, bf16[256,512]{1,0:T(8,128)(2,1)} %get-tuple-element.5.w_low, f32[128,2,24,128]{3,2,1,0:T(8,128)} %bitcast.25), custom_call_target="tpu_custom_call" | custom-call | tf_op jit(solution)/shard_map/pallas_call | solution.py:153
  199.3 53.9 %all-to-all-done.1 = f32[1,128,2,40,128]{4,3,2,0,1:T(8,128)} async-done(((f32[1,128,2,40,128]{4,3,2,0,1:T(8,128)}), f32[1,128,2,40,128]{4,3,2,0,1:T(8,128)}, u32[]{:S(2)}, u32[]{:S(2)}) %all-to-all-start.1) | async-done | bytes 5242912 | tf_op jit(solution)/shard_map/all_to_all | solution.py:191
  253.2 8.9 %shard_map.31 = bf16[64,128,512]{2,1,0:T(8,128)(2,1)} custom-call(bf16[256,512]{1,0:T(8,128)(2,1)} %get-tuple-element.6.w_high, bf16[256,512]{1,0:T(8,128)(2,1)} %get-tuple-element.5.w_low, f32[128,2,40,128]{3,2,1,0:T(8,128)} %bitcast.8.x_ref, bf16[64,128,512]{2,1,0:T(8,128)(2,1)} %shard_map.30.previous_ref), custom_call_target="tpu_custom_call", output_to_operand_aliasing={{}: (3, {})} | custom-call | tf_op jit(solution)/shard_map/pallas_call | solution.py:153
  (2 shorter events, 0.0 us)
Async XLA Ops:
  135.5 44.3 %all-to-all-start.2 = ((f32[1,128,2,24,128]{4,3,2,0,1:T(8,128)}), f32[1,128,2,24,128]{4,3,2,0,1:T(8,128)S(1)}, u32[]{:S(2)}, u32[]{:S(2)}) async-start(f32[1,128,2,24,128]{4,3,2,0,1:T(8,128)} %bitcast.26), calls=%async_computation.2 | async-start | bytes 6291456 | tf_op jit(solution)/shard_map/all_to_all | solution.py:191
  179.8 13.3 %copy-start = (f32[1,128,2,24,128]{4,3,2,0,1:T(8,128)}, f32[1,128,2,24,128]{4,3,2,0,1:T(8,128)S(1)}, u32[]{:S(2)}) copy-start(f32[1,128,2,24,128]{4,3,2,0,1:T(8,128)S(1)} %all-to-all-done.2) | copy-start | bytes 9437188
  179.8 73.4 %all-to-all-start.1 = ((f32[1,128,2,40,128]{4,3,2,0,1:T(8,128)}), f32[1,128,2,40,128]{4,3,2,0,1:T(8,128)}, u32[]{:S(2)}, u32[]{:S(2)}) async-start(f32[1,128,2,40,128]{4,3,2,0,1:T(8,128)} %bitcast.24), calls=%async_computation.1 | async-start | bytes 10485760 | tf_op jit(solution)/shard_map/all_to_all | solution.py:191

commit v9 on v8

--- a/solution.py
+++ b/solution.py
@@ -133,8 +133,8 @@
 def inverse_transform(home, inverse, first, total, previous):
     n_bins, _, span, cols = home.shape
     steps = inverse.shape[-1]
-    table = inverse.reshape(n_bins * 2, steps)
-    w_high, w_low = split_outside(table)
+    with jax.ensure_compile_time_eval():
+        w_high, w_low = split_outside(inverse.reshape(n_bins * 2, steps))
     group = 8
     offset = first // group
     operands = [w_high, w_low, home]
@@ -166,9 +166,8 @@
 
 
 def per_device(traces):
-    _, inverse = make_tables(NT, NF)
     with jax.ensure_compile_time_eval():
-        forward = make_tables(NT, NF)[0]
+        forward, inverse = make_tables(NT, NF)
     spectra = jnp.einsum(
         "srt,tpb->bpsr",
         traces.astype(jnp.float32),

time: 263 us -> 263 us (level)
  waiting for transfers between devices: 75.2 us -> 81.7 us
  local copies, waits for them, and re-layouts: 8.25 us -> 4.86 us
  other arithmetic: 3.07 us -> 0 us
    all_to_all x2, waiting for transfers between devices: 75.2 us -> 81.7 us  [per_device(): lax.all_to_all(pred.reshape(1, n_shot * n_freq, 2, span, cols), ('shot',...]
    div x2 -> x0, local copies, waits for them, and re-layouts: 3.39 us -> none  [make_tables(): jnp.stack([cosine.T, -sine.T], axis=1) / jnp.sqrt(jnp.float32(count_f))]
  transfers between devices with their start and end apart: 2 -> 2, of which waited for: 2 -> 2; matrix products, arithmetic and copies ran while one was open for 2% -> 0% of each run, Pallas kernels for 9% -> 9%
where the time goes in v9:
time: 263 us; the launch traced here: 262 us
  blocking collectives  110 us (42%)
  waiting for transfers between devices  81.7 us (31%)
  Pallas kernels  46.7 us (18%)
  starting transfers between devices  11.5 us (4%)
  matrix products  7.4 us (3%)
  local copies, waits for them, and re-layouts  4.86 us (2%)
    all_to_all x1, blocking collectives, per_device(): lax.all_to_all(spectra[None], ('shot', 'freq'), split_axis=1, concat_axis...  110 us
    all_to_all x2, waiting for transfers between devices, per_device(): lax.all_to_all(pred.reshape(1, n_shot * n_freq, 2, span, cols), ('shot',...  81.7 us
    pallas_call x2, Pallas kernels, complex_square(): pl.pallas_call(kernel, out_shape=jax.ShapeDtypeStruct((n_shot, n_freq, 2,...  31.6 us
    pallas_call x2, Pallas kernels, inverse_transform(): pl.pallas_call(kernel, out_shape=jax.ShapeDtypeStruct((total, cols, steps...  15.1 us
    all_to_all x2, starting transfers between devices, per_device(): lax.all_to_all(pred.reshape(1, n_shot * n_freq, 2, span, cols), ('shot',...  11.5 us
    dot_general x1, matrix products, per_device(): jnp.einsum('srt,tpb->bpsr', traces.astype(jnp.float32), forward, precisio...  7.4 us
  transfers between devices with their start and end apart: 2, of which 2 were waited for; matrix products, arithmetic and copies ran while one was open for 0% of the time, Pallas kernels for 9%

profile of v9, /device:TPU:6, one launch (start us, length us, event | category | flops | bytes accessed | tf_op | source)
XLA Modules:
  0.0 262.1 jit_solution(3487884517367424644)
XLA Ops:
  0.0 7.4 %fusion.2 = f32[1,128,2,64,128]{4,1,3,2,0:T(8,128)S(1)} fusion(f32[512,2,128,1]{0,2,3,1:T(8,128)} %constant.9, bf16[64,128,512]{2,1,0:T(8,128)(2,1)} %param.6), kind=kOutput, calls=%fused_computation.2 | convolution fusion | flops 6442450944 | bytes 17301504 | tf_op jit(solution)/shard_map/srt,tpb->bpsr/dot_general | solution.py:171
  7.4 4.9 %copy.9 = f32[1,128,2,64,128]{4,3,2,0,1:T(8,128)S(1)} copy(f32[1,128,2,64,128]{4,1,3,2,0:T(8,128)S(1)} %fusion.2) | data formatting | bytes 16777216 | tf_op jit(solution)/shard_map/broadcast_in_dim | solution.py:182
  12.3 109.9 %all_to_all.12 = f32[1,128,2,64,128]{4,3,2,0,1:T(8,128)} all-to-all(f32[1,128,2,64,128]{4,3,2,0,1:T(8,128)S(1)} %copy.9), channel_id=1, replica_groups=mesh['shot'=16,'freq'=8] {'shot','freq'}, dimensions={1} | all-to-all | bytes 16777216 | tf_op jit(solution)/shard_map/all_to_all | solution.py:182
  122.1 13.3 %shard_map.65 = f32[16,8,2,24,128]{4,3,2,1,0:T(8,128)} custom-call(f32[16,8,2,64,128]{4,3,2,1,0:T(8,128)} %bitcast.22), custom_call_target="tpu_custom_call" | custom-call | tf_op jit(solution)/shard_map/pallas_call | solution.py:103
  135.5 4.7 %all-to-all-start.2 = ((f32[1,128,2,24,128]{4,3,2,0,1:T(8,128)}), f32[1,128,2,24,128]{4,3,2,0,1:T(8,128)S(1)}, u32[]{:S(2)}, u32[]{:S(2)}) async-start(f32[1,128,2,24,128]{4,3,2,0,1:T(8,128)} %bitcast.26), calls=%async_computation.2 | async-start | bytes 6291456 | tf_op jit(solution)/shard_map/all_to_all | solution.py:190
  140.2 18.3 %shard_map.64 = f32[16,8,2,40,128]{4,3,2,1,0:T(8,128)} custom-call(f32[16,8,2,64,128]{4,3,2,1,0:T(8,128)} %bitcast.23), custom_call_target="tpu_custom_call" | custom-call | tf_op jit(solution)/shard_map/pallas_call | solution.py:103
  158.5 21.3 %all-to-all-done.2 = f32[1,128,2,24,128]{4,3,2,0,1:T(8,128)S(1)} async-done(((f32[1,128,2,24,128]{4,3,2,0,1:T(8,128)}), f32[1,128,2,24,128]{4,3,2,0,1:T(8,128)S(1)}, u32[]{:S(2)}, u32[]{:S(2)}) %all-to-all-start.2) | async-done | bytes 3145760 | tf_op jit(solution)/shard_map/all_to_all | solution.py:190
  179.8 0.0 copy-start
  179.8 6.8 %all-to-all-start.1 = ((f32[1,128,2,40,128]{4,3,2,0,1:T(8,128)}), f32[1,128,2,40,128]{4,3,2,0,1:T(8,128)}, u32[]{:S(2)}, u32[]{:S(2)}) async-start(f32[1,128,2,40,128]{4,3,2,0,1:T(8,128)} %bitcast.24), calls=%async_computation.1 | async-start | bytes 10485760 | tf_op jit(solution)/shard_map/all_to_all | solution.py:190
  186.6 0.0 copy-done
  186.6 6.2 %shard_map.66.previous_ref = bf16[64,128,512]{2,1,0:T(8,128)(2,1)} custom-call(bf16[256,512]{1,0:T(8,128)(2,1)} %constant.7.clone.w_high, bf16[256,512]{1,0:T(8,128)(2,1)} %constant.8.clone.w_low, f32[128,2,24,128]{3,2,1,0:T(8,128)} %bitcast.25), custom_call_target="tpu_custom_call" | custom-call | tf_op jit(solution)/shard_map/pallas_call | solution.py:153
  192.8 60.4 %all-to-all-done.1 = f32[1,128,2,40,128]{4,3,2,0,1:T(8,128)} async-done(((f32[1,128,2,40,128]{4,3,2,0,1:T(8,128)}), f32[1,128,2,40,128]{4,3,2,0,1:T(8,128)}, u32[]{:S(2)}, u32[]{:S(2)}) %all-to-all-start.1) | async-done | bytes 5242912 | tf_op jit(solution)/shard_map/all_to_all | solution.py:190
  253.2 8.9 %shard_map.67 = bf16[64,128,512]{2,1,0:T(8,128)(2,1)} custom-call(bf16[256,512]{1,0:T(8,128)(2,1)} %constant.7.clone.w_high, bf16[256,512]{1,0:T(8,128)(2,1)} %constant.8.clone.w_low, f32[128,2,40,128]{3,2,1,0:T(8,128)} %bitcast.8.x_ref, bf16[64,128,512]{2,1,0:T(8,128)(2,1)} %shard_map.66.previous_ref), custom_call_target="tpu_custom_call", output_to_operand_aliasing={{}: (3, {})} | custom-call | tf_op jit(solution)/shard_map/pallas_call | solution.py:153
Async XLA Ops:
  135.5 44.3 %all-to-all-start.2 = ((f32[1,128,2,24,128]{4,3,2,0,1:T(8,128)}), f32[1,128,2,24,128]{4,3,2,0,1:T(8,128)S(1)}, u32[]{:S(2)}, u32[]{:S(2)}) async-start(f32[1,128,2,24,128]{4,3,2,0,1:T(8,128)} %bitcast.26), calls=%async_computation.2 | async-start | bytes 6291456 | tf_op jit(solution)/shard_map/all_to_all | solution.py:190
  179.8 6.9 %copy-start = (f32[1,128,2,24,128]{4,3,2,0,1:T(8,128)}, f32[1,128,2,24,128]{4,3,2,0,1:T(8,128)S(1)}, u32[]{:S(2)}) copy-start(f32[1,128,2,24,128]{4,3,2,0,1:T(8,128)S(1)} %all-to-all-done.2) | copy-start | bytes 9437188
  179.8 73.4 %all-to-all-start.1 = ((f32[1,128,2,40,128]{4,3,2,0,1:T(8,128)}), f32[1,128,2,40,128]{4,3,2,0,1:T(8,128)}, u32[]{:S(2)}, u32[]{:S(2)}) async-start(f32[1,128,2,40,128]{4,3,2,0,1:T(8,128)} %bitcast.24), calls=%async_computation.1 | async-start | bytes 10485760 | tf_op jit(solution)/shard_map/all_to_all | solution.py:190
